TPU v7x, 128 devices: a whole 4x4x4 slice. The times are simulated.
128 devices in a mesh: seq: 128 (over y, x, z, core).
Axes of the slice: x: 4, y: 4, z: 4, core: 2. Of those that a mesh axis runs over, the one named last changes fastest.
Arguments:
- queries: bfloat16 [16384, 8192], P('seq'), may hold values from -5.1 to 5.1
- keys: bfloat16 [16384, 1024], P('seq'), may hold values from -5.1 to 5.1
- values: bfloat16 [16384, 1024], P('seq'), may hold values from -6 to 6
- lengths: int32 [32], replicated, may hold values from 1 to 8, 128 in all
- class_weight: bfloat16 [8192, 16], replicated, may hold values from -0.25 to 0.25
Outputs:
- attended: bfloat16 [16384, 8192], P('seq')
- doc_logits: float32 [128, 16], P('seq')
Inputs may be any that keep to these rules, and one draw needn't show every extreme that they name: `lengths`: lengths are counted in blocks of 128 tokens; they sum to 128 and the longest is exactly 8 blocks.
All inputs are finite; a program needn't handle non-finite values.
Results may differ from a plain program's by a relative error of at most 0.0046.
Values may be sent and summed in bfloat16 or wider, within the bound.
No kernel may reach another device: no remote copies, remote signals or barrier semaphores. Data moves between devices by JAX's collectives and lax.ppermute only.
A program may use at most 192 MiB of HBM per device.

v0:
```python
import jax
import jax.numpy as jnp
from jax import lax
from jax.sharding import PartitionSpec as P
from jax.experimental import pallas as pl
from jax.experimental.pallas import tpu as pltpu

DH = 128
BLK = 128
MAXB = 8


def shifted(block, axis, distance):
    count = lax.axis_size(axis)
    if distance > 0:
        route = [(i - distance, i) for i in range(distance, count)]
    else:
        route = [(i - distance, i) for i in range(0, count + distance)]
    return lax.ppermute(block, axis, route)


def block_docs(lengths, block_count):
    doc_ends = jnp.cumsum(lengths, dtype=jnp.int32)
    doc_firsts = doc_ends - lengths
    blocks = jnp.arange(block_count, dtype=jnp.int32)
    owner_doc = jnp.sum((doc_ends[None, :] <= blocks[:, None]).astype(jnp.int32), axis=1)
    matches = owner_doc[:, None] == jnp.arange(lengths.shape[0], dtype=jnp.int32)[None, :]
    first_block = jnp.sum(jnp.where(matches, doc_firsts[None, :], 0), axis=1)
    return (owner_doc, first_block)


def attention_kernel(flags_ref, q_ref, *refs):
    kv_refs = refs[:-1]
    out_ref = refs[-1]
    width_k = kv_refs[0].shape[1] // 2
    heads = q_ref.shape[1] // DH
    group = heads // (width_k // DH)
    factor = DH ** (-0.5)

    def one_head(j, carry):
        qcol = pl.multiple_of(j * DH, DH)
        kcol = pl.multiple_of((j // group) * DH, DH)
        vcol = pl.multiple_of(width_k + (j // group) * DH, DH)
        q = q_ref[:, pl.ds(qcol, DH)]

        def tile(kv_ref):
            k = kv_ref[:, pl.ds(kcol, DH)]
            v = kv_ref[:, pl.ds(vcol, DH)]
            s = (
                lax.dot_general(q, k, (((1,), (1,)), ((), ())), preferred_element_type=jnp.float32)
                * factor
            )
            m = jnp.max(s, axis=1, keepdims=True)
            p = jnp.exp(s - m)
            l = jnp.sum(p, axis=1, keepdims=True)
            o = jnp.dot(p.astype(jnp.bfloat16), v, preferred_element_type=jnp.float32)
            return m, l, o

        state = tile(kv_refs[0])
        for t in range(1, len(kv_refs)):

            def take(state, kv_ref=kv_refs[t]):
                m0, l0, o0 = state
                m1, l1, o1 = tile(kv_ref)
                mn = jnp.maximum(m0, m1)
                a = jnp.exp(m0 - mn)
                b = jnp.exp(m1 - mn)
                return mn, l0 * a + l1 * b, o0 * a + o1 * b

            state = lax.cond(flags_ref[t] > 0, take, lambda s: s, state)
        m, l, o = state
        out_ref[:, pl.ds(qcol, DH)] = (o / l).astype(out_ref.dtype)
        return carry

    lax.fori_loop(0, heads, one_head, 0)


def attend(flags, queries, pieces):
    return pl.pallas_call(
        attention_kernel,
        out_shape=jax.ShapeDtypeStruct(queries.shape, jnp.bfloat16),
        in_specs=[pl.BlockSpec(memory_space=pltpu.SMEM)]
        + [pl.BlockSpec(memory_space=pltpu.VMEM)] * (1 + len(pieces)),
        out_specs=pl.BlockSpec(memory_space=pltpu.VMEM),
        compiler_params=pltpu.CompilerParams(vmem_limit_bytes=48 * 1024 * 1024),
    )(flags, queries, *pieces)


def shards(queries, keys, values, lengths, class_weight):
    devices = lax.axis_size("seq")
    myself = lax.axis_index("seq")
    row_count = queries.shape[0]
    run_rows = row_count // devices
    width_q = queries.shape[1]
    width_k = keys.shape[1]
    arrived_q = lax.all_to_all(
        queries.reshape(devices, run_rows, width_q), "seq", split_axis=0, concat_axis=0, tiled=True
    )
    arrived_kv = lax.all_to_all(
        jnp.concatenate([keys, values], axis=1).reshape(devices, run_rows, 2 * width_k),
        "seq",
        split_axis=0,
        concat_axis=0,
        tiled=True,
    )
    queries = arrived_q.reshape(row_count, width_q)
    kv = arrived_kv.reshape(row_count, 2 * width_k)
    owner_doc, first_block = block_docs(lengths, devices)
    my_doc = owner_doc[myself]
    reach = MAXB - 1
    pieces = [kv]
    flags = [jnp.ones((), jnp.int32)]
    right = kv
    left = kv
    for hop in range(1, reach + 1):
        right = shifted(right, "seq", 1)
        left = shifted(left, "seq", -1)
        for piece, source in ((right, myself - hop), (left, myself + hop)):
            inside = (source >= 0) & (source < devices)
            clipped = jnp.clip(source, 0, devices - 1)
            pieces.append(piece)
            flags.append((inside & (owner_doc[clipped] == my_doc)).astype(jnp.int32))
    attended = attend(jnp.stack(flags), queries, pieces)
    own_logits = jnp.dot(attended[0:1], class_weight, preferred_element_type=jnp.float32)
    candidates = [own_logits] + [shifted(own_logits, "seq", d) for d in range(1, reach + 1)]
    distance = jnp.clip(myself - first_block[myself], 0, reach)
    doc_logits = lax.dynamic_index_in_dim(jnp.stack(candidates), distance, 0, False)
    return (attended, doc_logits)


def solution(mesh):
    return jax.shard_map(
        shards,
        mesh=mesh,
        in_specs=(P("seq", None), P("seq", None), P("seq", None), P(), P()),
        out_specs=(P("seq", None), P("seq", None)),
        check_vma=False,
    )
```

profile of v0, /device:TPU:9, one launch (start us, length us, event | category | flops | bytes accessed | tf_op | source)
XLA Modules:
  0.0 428.0 jit_solution(1420599227284121682)
XLA Ops:
  3.6 23.0 %all_to_all.10 = bf16[128,2,1024]{2,1,0:T(2,128)(2,1)S(1)} all-to-all(bf16[128,2,1024]{2,1,0:T(2,128)(2,1)S(1)} %reshape.73), channel_id=1, replica_groups=mesh['seq'=128] {'seq'}, dimensions={0} | all-to-all | bytes 1048576 | tf_op jit(solution)/shard_map/all_to_all | solution.py:99
  29.3 3.2 collective-permute-start.1
  32.5 2.9 collective-permute-done.refs_1_
  35.4 4.4 %collective-permute-start.2 = (bf16[128,2048]{1,0:T(8,128)(2,1)S(1)}, bf16[128,2048]{1,0:T(8,128)(2,1)S(1)}, u32[]{:S(2)}, u32[]{:S(2)}) collective-permute-start(bf16[128,2048]{1,0:T(8,128)(2,1)S(1)} %collective-permute-done.refs_1_), channel_id=1, source_target_pairs={{0,1},{1,2},{2,3},{3,4},{4,5},{5,6},{6,7},{7,8},{8,9},{9,10},{10,1... | collective-permute-start | bytes 1572872 | tf_op jit(solution)/shard_map/ppermute | solution.py:19
  40.1 7.1 %collective-permute-start.3 = (bf16[128,2048]{1,0:T(8,128)(2,1)S(1)}, bf16[128,2048]{1,0:T(8,128)(2,1)S(1)}, u32[]{:S(2)}, u32[]{:S(2)}) collective-permute-start(bf16[128,2048]{1,0:T(8,128)(2,1)S(1)} %collective-permute-done.1.refs_2_), channel_id=1, source_target_pairs={{1,0},{2,1},{3,2},{4,3},{5,4},{6,5},{7,6},{8,7},{9,8},{10,9},{11,1... | collective-permute-start | bytes 1572872 | tf_op jit(solution)/shard_map/ppermute | solution.py:19
  47.3 3.0 collective-permute-start.4
  50.6 11.4 %collective-permute-start.5 = (bf16[128,2048]{1,0:T(8,128)(2,1)S(1)}, bf16[128,2048]{1,0:T(8,128)(2,1)}, u32[]{:S(2)}, u32[]{:S(2)}) collective-permute-start(bf16[128,2048]{1,0:T(8,128)(2,1)S(1)} %collective-permute-done.3.refs_4_), channel_id=1, source_target_pairs={{1,0},{2,1},{3,2},{4,3},{5,4},{6,5},{7,6},{8,7},{9,8},{10,9},{11,1... | collective-permute-start | bytes 1572872 | tf_op jit(solution)/shard_map/ppermute | solution.py:19
  63.9 12.8 %collective-permute-start.7 = (bf16[128,2048]{1,0:T(8,128)(2,1)}, bf16[128,2048]{1,0:T(8,128)(2,1)}, u32[]{:S(2)}, u32[]{:S(2)}) collective-permute-start(bf16[128,2048]{1,0:T(8,128)(2,1)} %collective-permute-done.5.refs_6_), channel_id=1, source_target_pairs={{1,0},{2,1},{3,2},{4,3},{5,4},{6,5},{7,6},{8,7},{9,8},{10,9},{11,1... | collective-permute-start | bytes 1572872 | tf_op jit(solution)/shard_map/ppermute | solution.py:19
  76.7 4.5 %reduce.1 = bf16[128,8192]{1,0:T(8,128)(2,1)} reduce(bf16[128,1,8192]{2,0,1:T(8,128)(2,1)} %bitcast.69, bf16[]{:T(256)} %broadcast.3), dimensions={1}, to_apply=%copy.14.reduce_sub_computation | reduce | bytes 4194306 | tf_op jit(solution)/shard_map/reshape | solution.py:97
  81.2 4.5 %reshape.71 = bf16[128,2,4096]{2,1,0:T(2,128)(2,1)} reshape(bf16[128,8192]{1,0:T(8,128)(2,1)} %reduce.1) | data formatting | bytes 4194304
  85.7 9.5 %all-to-all-start = ((bf16[128,2,4096]{2,1,0:T(2,128)(2,1)}), bf16[128,2,4096]{2,1,0:T(2,128)(2,1)}, u32[]{:S(2)}, u32[]{:S(2)}) async-start(bf16[128,2,4096]{2,1,0:T(2,128)(2,1)} %reshape.71), calls=%async_computation | async-start | bytes 4194304 | tf_op jit(solution)/shard_map/all_to_all | solution.py:96
  95.2 3.6 collective-permute-start.8
  100.7 22.9 %collective-permute-done.8.refs_9_ = bf16[128,2048]{1,0:T(8,128)(2,1)S(1)} collective-permute-done((bf16[128,2048]{1,0:T(8,128)(2,1)}, bf16[128,2048]{1,0:T(8,128)(2,1)S(1)}, u32[]{:S(2)}, u32[]{:S(2)}) %collective-permute-start.8) | collective-permute-done | bytes 524320 | tf_op jit(solution)/shard_map/ppermute | solution.py:19
  123.6 4.3 collective-permute-start.10
  128.7 5.4 %collective-permute-start.11 = (bf16[128,2048]{1,0:T(8,128)(2,1)S(1)}, bf16[128,2048]{1,0:T(8,128)(2,1)}, u32[]{:S(2)}, u32[]{:S(2)}) collective-permute-start(bf16[128,2048]{1,0:T(8,128)(2,1)S(1)} %collective-permute-done.9.refs_10_), channel_id=1, source_target_pairs={{1,0},{2,1},{3,2},{4,3},{5,4},{6,5},{7,6},{8,7},{9,8},{10,9},{11,1... | collective-permute-start | bytes 1572872 | tf_op jit(solution)/shard_map/ppermute | solution.py:19
  134.9 3.6 collective-permute-start.12
  139.6 9.0 %collective-permute-start.13 = (bf16[128,2048]{1,0:T(8,128)(2,1)}, bf16[128,2048]{1,0:T(8,128)(2,1)}, u32[]{:S(2)}, u32[]{:S(2)}) collective-permute-start(bf16[128,2048]{1,0:T(8,128)(2,1)} %collective-permute-done.11.refs_12_), channel_id=1, source_target_pairs={{1,0},{2,1},{3,2},{4,3},{5,4},{6,5},{7,6},{8,7},{9,8},{10,9},{11,1... | collective-permute-start | bytes 1572872 | tf_op jit(solution)/shard_map/ppermute | solution.py:19
  169.0 13.8 %reshape.72 = bf16[128,1,8192]{2,1,0:T(2,128)(2,1)} reshape(bf16[128,2,4096]{2,1,0:T(2,128)(2,1)} %all-to-all-done) | data formatting | bytes 4194304
  182.9 5.9 %copy.20 = bf16[128,1,8192]{2,0,1:T(8,128)(2,1)} copy(bf16[128,1,8192]{2,1,0:T(2,128)(2,1)} %reshape.72) | data formatting | bytes 4194304
  188.8 210.3 %shard_map.68 = bf16[128,8192]{1,0:T(8,128)(2,1)} custom-call(s32[15]{0:T(128)S(1)} %stack.103.flags_ref, bf16[128,8192]{1,0:T(8,128)(2,1)} %bitcast.68, bf16[128,2048]{1,0:T(8,128)(2,1)S(1)} %bitcast.67, bf16[128,2048]{1,0:T(8,128)(2,1)S(1)} %collective-permute-done.refs_1_, bf16[128,2048]{1,0:T(8,128)(2,1)S(1)} %collective-permute-done.1.refs_2_, ...), custom_call_target="tpu_custom_call" | custom-call | tf_op jit(solution)/shard_map/pallas_call | solution.py:79
  404.0 3.7 collective-permute-start.16
  413.5 2.9 collective-permute-done.15
  418.9 2.5 collective-permute-done.17
  424.9 2.5 collective-permute-done.20
  (63 shorter events, 32.0 us)
Async XLA Ops:
  0.6 398.4 %copy-start = (bf16[8192,16]{0,1:T(8,128)(2,1)S(1)}, bf16[8192,16]{0,1:T(8,128)(2,1)}, u32[]{:S(2)}) copy-start(bf16[8192,16]{0,1:T(8,128)(2,1)} %param.9) | copy-start | bytes 786436
  27.4 8.0 %collective-permute-start = (bf16[128,2048]{1,0:T(8,128)(2,1)S(1)}, bf16[128,2048]{1,0:T(8,128)(2,1)S(1)}, u32[]{:S(2)}, u32[]{:S(2)}) collective-permute-start(bf16[128,2048]{1,0:T(8,128)(2,1)S(1)} %bitcast.65), channel_id=1, source_target_pairs={{0,1},{1,2},{2,3},{3,4},{4,5},{5,6},{6,7},{7,8},{8,9},{9,10},{10,1... | collective-permute-start | bytes 1572872 | tf_op jit(solution)/shard_map/ppermute | solution.py:19
  29.3 10.8 %collective-permute-start.1 = (bf16[128,2048]{1,0:T(8,128)(2,1)S(1)}, bf16[128,2048]{1,0:T(8,128)(2,1)S(1)}, u32[]{:S(2)}, u32[]{:S(2)}) collective-permute-start(bf16[128,2048]{1,0:T(8,128)(2,1)S(1)} %bitcast.66), channel_id=1, source_target_pairs={{1,0},{2,1},{3,2},{4,3},{5,4},{6,5},{7,6},{8,7},{9,8},{10,9},{11,1... | collective-permute-start | bytes 1572872 | tf_op jit(solution)/shard_map/ppermute | solution.py:19
  35.4 11.8 %collective-permute-start.2 = (bf16[128,2048]{1,0:T(8,128)(2,1)S(1)}, bf16[128,2048]{1,0:T(8,128)(2,1)S(1)}, u32[]{:S(2)}, u32[]{:S(2)}) collective-permute-start(bf16[128,2048]{1,0:T(8,128)(2,1)S(1)} %collective-permute-done.refs_1_), channel_id=1, source_target_pairs={{0,1},{1,2},{2,3},{3,4},{4,5},{5,6},{6,7},{7,8},{8,9},{9,10},{10,1... | collective-permute-start | bytes 1572872 | tf_op jit(solution)/shard_map/ppermute | solution.py:19
  40.1 10.5 %collective-permute-start.3 = (bf16[128,2048]{1,0:T(8,128)(2,1)S(1)}, bf16[128,2048]{1,0:T(8,128)(2,1)S(1)}, u32[]{:S(2)}, u32[]{:S(2)}) collective-permute-start(bf16[128,2048]{1,0:T(8,128)(2,1)S(1)} %collective-permute-done.1.refs_2_), channel_id=1, source_target_pairs={{1,0},{2,1},{3,2},{4,3},{5,4},{6,5},{7,6},{8,7},{9,8},{10,9},{11,1... | collective-permute-start | bytes 1572872 | tf_op jit(solution)/shard_map/ppermute | solution.py:19
  47.3 14.7 %collective-permute-start.4 = (bf16[128,2048]{1,0:T(8,128)(2,1)S(1)}, bf16[128,2048]{1,0:T(8,128)(2,1)S(1)}, u32[]{:S(2)}, u32[]{:S(2)}) collective-permute-start(bf16[128,2048]{1,0:T(8,128)(2,1)S(1)} %collective-permute-done.2.refs_3_), channel_id=1, source_target_pairs={{0,1},{1,2},{2,3},{3,4},{4,5},{5,6},{6,7},{7,8},{8,9},{9,10},{10,1... | collective-permute-start | bytes 1572872 | tf_op jit(solution)/shard_map/ppermute | solution.py:19
  50.6 13.3 %collective-permute-start.5 = (bf16[128,2048]{1,0:T(8,128)(2,1)S(1)}, bf16[128,2048]{1,0:T(8,128)(2,1)}, u32[]{:S(2)}, u32[]{:S(2)}) collective-permute-start(bf16[128,2048]{1,0:T(8,128)(2,1)S(1)} %collective-permute-done.3.refs_4_), channel_id=1, source_target_pairs={{1,0},{2,1},{3,2},{4,3},{5,4},{6,5},{7,6},{8,7},{9,8},{10,9},{11,1... | collective-permute-start | bytes 1572872 | tf_op jit(solution)/shard_map/ppermute | solution.py:19
  62.0 33.2 %collective-permute-start.6 = (bf16[128,2048]{1,0:T(8,128)(2,1)S(1)}, bf16[128,2048]{1,0:T(8,128)(2,1)}, u32[]{:S(2)}, u32[]{:S(2)}) collective-permute-start(bf16[128,2048]{1,0:T(8,128)(2,1)S(1)} %collective-permute-done.4.refs_5_), channel_id=1, source_target_pairs={{0,1},{1,2},{2,3},{3,4},{4,5},{5,6},{6,7},{7,8},{8,9},{9,10},{10,1... | collective-permute-start | bytes 1572872 | tf_op jit(solution)/shard_map/ppermute | solution.py:19
  63.9 34.8 %collective-permute-start.7 = (bf16[128,2048]{1,0:T(8,128)(2,1)}, bf16[128,2048]{1,0:T(8,128)(2,1)}, u32[]{:S(2)}, u32[]{:S(2)}) collective-permute-start(bf16[128,2048]{1,0:T(8,128)(2,1)} %collective-permute-done.5.refs_6_), channel_id=1, source_target_pairs={{1,0},{2,1},{3,2},{4,3},{5,4},{6,5},{7,6},{8,7},{9,8},{10,9},{11,1... | collective-permute-start | bytes 1572872 | tf_op jit(solution)/shard_map/ppermute | solution.py:19
  85.7 63.0 %copy-start.5 = (s32[32]{0:T(128)S(1)}, s32[32]{0:T(128)}, u32[]{:S(2)}) copy-start(s32[32]{0:T(128)} %param.8) | copy-start | bytes 388
  85.7 83.3 %all-to-all-start = ((bf16[128,2,4096]{2,1,0:T(2,128)(2,1)}), bf16[128,2,4096]{2,1,0:T(2,128)(2,1)}, u32[]{:S(2)}, u32[]{:S(2)}) async-start(bf16[128,2,4096]{2,1,0:T(2,128)(2,1)} %reshape.71), calls=%async_computation | async-start | bytes 4194304 | tf_op jit(solution)/shard_map/all_to_all | solution.py:96
  95.2 28.4 %collective-permute-start.8 = (bf16[128,2048]{1,0:T(8,128)(2,1)}, bf16[128,2048]{1,0:T(8,128)(2,1)S(1)}, u32[]{:S(2)}, u32[]{:S(2)}) collective-permute-start(bf16[128,2048]{1,0:T(8,128)(2,1)} %collective-permute-done.6.refs_7_), channel_id=1, source_target_pairs={{0,1},{1,2},{2,3},{3,4},{4,5},{5,6},{6,7},{7,8},{8,9},{9,10},{10,1... | collective-permute-start | bytes 1572872 | tf_op jit(solution)/shard_map/ppermute | solution.py:19
  98.7 29.9 %collective-permute-start.9 = (bf16[128,2048]{1,0:T(8,128)(2,1)}, bf16[128,2048]{1,0:T(8,128)(2,1)S(1)}, u32[]{:S(2)}, u32[]{:S(2)}) collective-permute-start(bf16[128,2048]{1,0:T(8,128)(2,1)} %collective-permute-done.7.refs_8_), channel_id=1, source_target_pairs={{1,0},{2,1},{3,2},{4,3},{5,4},{6,5},{7,6},{8,7},{9,8},{10,9},{11,1... | collective-permute-start | bytes 1572872 | tf_op jit(solution)/shard_map/ppermute | solution.py:19
  123.6 11.3 %collective-permute-start.10 = (bf16[128,2048]{1,0:T(8,128)(2,1)S(1)}, bf16[128,2048]{1,0:T(8,128)(2,1)}, u32[]{:S(2)}, u32[]{:S(2)}) collective-permute-start(bf16[128,2048]{1,0:T(8,128)(2,1)S(1)} %collective-permute-done.8.refs_9_), channel_id=1, source_target_pairs={{0,1},{1,2},{2,3},{3,4},{4,5},{5,6},{6,7},{7,8},{8,9},{9,10},{10,1... | collective-permute-start | bytes 1572872 | tf_op jit(solution)/shard_map/ppermute | solution.py:19
  128.7 10.9 %collective-permute-start.11 = (bf16[128,2048]{1,0:T(8,128)(2,1)S(1)}, bf16[128,2048]{1,0:T(8,128)(2,1)}, u32[]{:S(2)}, u32[]{:S(2)}) collective-permute-start(bf16[128,2048]{1,0:T(8,128)(2,1)S(1)} %collective-permute-done.9.refs_10_), channel_id=1, source_target_pairs={{1,0},{2,1},{3,2},{4,3},{5,4},{6,5},{7,6},{8,7},{9,8},{10,9},{11,1... | collective-permute-start | bytes 1572872 | tf_op jit(solution)/shard_map/ppermute | solution.py:19
  134.9 53.9 %collective-permute-start.12 = (bf16[128,2048]{1,0:T(8,128)(2,1)}, bf16[128,2048]{1,0:T(8,128)(2,1)}, u32[]{:S(2)}, u32[]{:S(2)}) collective-permute-start(bf16[128,2048]{1,0:T(8,128)(2,1)} %collective-permute-done.10.refs_11_), channel_id=1, source_target_pairs={{0,1},{1,2},{2,3},{3,4},{4,5},{5,6},{6,7},{7,8},{8,9},{9,10},{10,1... | collective-permute-start | bytes 1572872 | tf_op jit(solution)/shard_map/ppermute | solution.py:19
  139.6 49.2 %collective-permute-start.13 = (bf16[128,2048]{1,0:T(8,128)(2,1)}, bf16[128,2048]{1,0:T(8,128)(2,1)}, u32[]{:S(2)}, u32[]{:S(2)}) collective-permute-start(bf16[128,2048]{1,0:T(8,128)(2,1)} %collective-permute-done.11.refs_12_), channel_id=1, source_target_pairs={{1,0},{2,1},{3,2},{4,3},{5,4},{6,5},{7,6},{8,7},{9,8},{10,9},{11,1... | collective-permute-start | bytes 1572872 | tf_op jit(solution)/shard_map/ppermute | solution.py:19
  400.1 11.4 %collective-permute-start.14 = (f32[1,16]{1,0:T(1,128)S(1)}, f32[1,16]{1,0:T(1,128)S(1)}, u32[]{:S(2)}, u32[]{:S(2)}) collective-permute-start(f32[1,16]{1,0:T(1,128)S(1)} %get-tuple-element.18), channel_id=1, source_target_pairs={{0,1},{1,2},{2,3},{3,4},{4,5},{5,6},{6,7},{7,8},{8,9},{9,10},{10,1... | collective-permute-start | bytes 200 | tf_op jit(solution)/shard_map/ppermute | solution.py:19
  402.1 14.3 %collective-permute-start.15 = (f32[1,16]{1,0:T(1,128)S(1)}, f32[1,16]{1,0:T(1,128)S(1)}, u32[]{:S(2)}, u32[]{:S(2)}) collective-permute-start(f32[1,16]{1,0:T(1,128)S(1)} %get-tuple-element.18), channel_id=1, source_target_pairs={{0,2},{1,3},{2,4},{3,5},{4,6},{5,7},{6,8},{7,9},{8,10},{9,11},{10,... | collective-permute-start | bytes 200 | tf_op jit(solution)/shard_map/ppermute | solution.py:19
  404.0 14.9 %collective-permute-start.16 = (f32[1,16]{1,0:T(1,128)S(1)}, f32[1,16]{1,0:T(1,128)S(1)}, u32[]{:S(2)}, u32[]{:S(2)}) collective-permute-start(f32[1,16]{1,0:T(1,128)S(1)} %get-tuple-element.18), channel_id=1, source_target_pairs={{0,3},{1,4},{2,5},{3,6},{4,7},{5,8},{6,9},{7,10},{8,11},{9,12},{10... | collective-permute-start | bytes 200 | tf_op jit(solution)/shard_map/ppermute | solution.py:19
  407.7 13.7 %collective-permute-start.17 = (f32[1,16]{1,0:T(1,128)S(1)}, f32[1,16]{1,0:T(1,128)S(1)}, u32[]{:S(2)}, u32[]{:S(2)}) collective-permute-start(f32[1,16]{1,0:T(1,128)S(1)} %get-tuple-element.18), channel_id=1, source_target_pairs={{0,4},{1,5},{2,6},{3,7},{4,8},{5,9},{6,10},{7,11},{8,12},{9,13},{1... | collective-permute-start | bytes 200 | tf_op jit(solution)/shard_map/ppermute | solution.py:19
  409.6 14.3 %collective-permute-start.18 = (f32[1,16]{1,0:T(1,128)S(1)}, f32[1,16]{1,0:T(1,128)S(1)}, u32[]{:S(2)}, u32[]{:S(2)}) collective-permute-start(f32[1,16]{1,0:T(1,128)S(1)} %get-tuple-element.18), channel_id=1, source_target_pairs={{0,5},{1,6},{2,7},{3,8},{4,9},{5,10},{6,11},{7,12},{8,13},{9,14},{... | collective-permute-start | bytes 200 | tf_op jit(solution)/shard_map/ppermute | solution.py:19
  411.6 13.4 %collective-permute-start.19 = (f32[1,16]{1,0:T(1,128)S(1)}, f32[1,16]{1,0:T(1,128)S(1)}, u32[]{:S(2)}, u32[]{:S(2)}) collective-permute-start(f32[1,16]{1,0:T(1,128)S(1)} %get-tuple-element.18), channel_id=1, source_target_pairs={{0,6},{1,7},{2,8},{3,9},{4,10},{5,11},{6,12},{7,13},{8,14},{9,15},... | collective-permute-start | bytes 200 | tf_op jit(solution)/shard_map/ppermute | solution.py:19
  416.4 11.1 %collective-permute-start.20 = (f32[1,16]{1,0:T(1,128)S(1)}, f32[1,16]{1,0:T(1,128)S(1)}, u32[]{:S(2)}, u32[]{:S(2)}) collective-permute-start(f32[1,16]{1,0:T(1,128)S(1)} %get-tuple-element.18), channel_id=1, source_target_pairs={{0,7},{1,8},{2,9},{3,10},{4,11},{5,12},{6,13},{7,14},{8,15},{9,16}... | collective-permute-start | bytes 200 | tf_op jit(solution)/shard_map/ppermute | solution.py:19
  (4 other events, 13.4 us)
where the time goes:
time: 432 us; the launch traced here: 428 us
  Pallas kernels  210 us (49%)
  starting transfers between devices  98.1 us (23%)
  waiting for transfers between devices  39.6 us (9%)
  local copies, waits for them, and re-layouts  29.6 us (7%)
  blocking collectives  23 us (5%)
  between operations  19.4 us (4%)
  other arithmetic  6.96 us (2%)
    pallas_call x1, Pallas kernels, attend(): pl.pallas_call(attention_kernel, out_shape=jax.ShapeDtypeStruct(queries.s...  210 us
    ppermute x21, starting transfers between devices, shifted(): return lax.ppermute(block, axis, route)  88.6 us
    ppermute x21, waiting for transfers between devices, shifted(): return lax.ppermute(block, axis, route)  39.5 us
    unnamed x24, local copies, waits for them, and re-layouts  27 us
    all_to_all x1, blocking collectives, shards(): lax.all_to_all(jnp.concatenate([keys, values], axis=1).reshape(devices, r...  23 us
    all_to_all x1, starting transfers between devices, shards(): lax.all_to_all(queries.reshape(devices, run_rows, width_q), 'seq', split_...  9.49 us
  transfers between devices with their start and end apart: 22, of which 11 were waited for; matrix products, arithmetic and copies ran while one was open for 7% of the time, Pallas kernels for 0%

commit v1 on v0

--- a/solution.py
+++ b/solution.py
@@ -30,59 +30,82 @@
 
 
 def attention_kernel(flags_ref, q_ref, *refs):
-    kv_refs = refs[:-1]
-    out_ref = refs[-1]
-    width_k = kv_refs[0].shape[1] // 2
-    heads = q_ref.shape[1] // DH
-    group = heads // (width_k // DH)
+    tiles = len(refs) - 5
+    kv_refs = refs[:tiles]
+    out_ref, qs_ref, m_ref, l_ref, acc_ref = refs[tiles:]
+    heads_kv = qs_ref.shape[0]
+    rows = q_ref.shape[0]
+    group = qs_ref.shape[1] // rows
+    width_k = heads_kv * DH
     factor = DH ** (-0.5)
+    for h in range(heads_kv):
+        for g in range(group):
+            qs_ref[h, g * rows : (g + 1) * rows, :] = q_ref[:, (h * group + g) * DH : (h * group + g + 1) * DH]
 
-    def one_head(j, carry):
-        qcol = pl.multiple_of(j * DH, DH)
-        kcol = pl.multiple_of((j // group) * DH, DH)
-        vcol = pl.multiple_of(width_k + (j // group) * DH, DH)
-        q = q_ref[:, pl.ds(qcol, DH)]
-
-        def tile(kv_ref):
+    def tile_step(kv_ref, first):
+        def one_head(h, carry):
+            kcol = pl.multiple_of(h * DH, DH)
+            vcol = pl.multiple_of(width_k + h * DH, DH)
             k = kv_ref[:, pl.ds(kcol, DH)]
             v = kv_ref[:, pl.ds(vcol, DH)]
             s = (
-                lax.dot_general(q, k, (((1,), (1,)), ((), ())), preferred_element_type=jnp.float32)
+                lax.dot_general(
+                    qs_ref[h], k, (((1,), (1,)), ((), ())), preferred_element_type=jnp.float32
+                )
                 * factor
             )
-            m = jnp.max(s, axis=1, keepdims=True)
-            p = jnp.exp(s - m)
-            l = jnp.sum(p, axis=1, keepdims=True)
-            o = jnp.dot(p.astype(jnp.bfloat16), v, preferred_element_type=jnp.float32)
-            return m, l, o
-
-        state = tile(kv_refs[0])
-        for t in range(1, len(kv_refs)):
-
-            def take(state, kv_ref=kv_refs[t]):
-                m0, l0, o0 = state
-                m1, l1, o1 = tile(kv_ref)
+            m1 = jnp.max(s, axis=1, keepdims=True)
+            p = jnp.exp(s - m1)
+            l1 = jnp.sum(p, axis=1, keepdims=True)
+            o1 = jnp.dot(p.astype(jnp.bfloat16), v, preferred_element_type=jnp.float32)
+            if first:
+                m_ref[h] = m1
+                l_ref[h] = l1
+                acc_ref[h] = o1
+            else:
+                m0 = m_ref[h]
                 mn = jnp.maximum(m0, m1)
                 a = jnp.exp(m0 - mn)
                 b = jnp.exp(m1 - mn)
-                return mn, l0 * a + l1 * b, o0 * a + o1 * b
+                m_ref[h] = mn
+                l_ref[h] = l_ref[h] * a + l1 * b
+                acc_ref[h] = acc_ref[h] * a + o1 * b
+            return carry
 
-            state = lax.cond(flags_ref[t] > 0, take, lambda s: s, state)
-        m, l, o = state
-        out_ref[:, pl.ds(qcol, DH)] = (o / l).astype(out_ref.dtype)
-        return carry
+        lax.fori_loop(0, heads_kv, one_head, 0)
 
-    lax.fori_loop(0, heads, one_head, 0)
+    tile_step(kv_refs[0], True)
+    for t in range(1, tiles):
+
+        @pl.when(flags_ref[t] > 0)
+        def _(kv_ref=kv_refs[t]):
+            tile_step(kv_ref, False)
+
+    for h in range(heads_kv):
+        normed = acc_ref[h] / l_ref[h]
+        for g in range(group):
+            out_ref[:, (h * group + g) * DH : (h * group + g + 1) * DH] = normed[
+                g * rows : (g + 1) * rows
+            ].astype(out_ref.dtype)
 
 
 def attend(flags, queries, pieces):
+    rows = queries.shape[0]
+    heads_kv = pieces[0].shape[1] // (2 * DH)
+    group = queries.shape[1] // (heads_kv * DH)
     return pl.pallas_call(
         attention_kernel,
         out_shape=jax.ShapeDtypeStruct(queries.shape, jnp.bfloat16),
         in_specs=[pl.BlockSpec(memory_space=pltpu.SMEM)]
         + [pl.BlockSpec(memory_space=pltpu.VMEM)] * (1 + len(pieces)),
         out_specs=pl.BlockSpec(memory_space=pltpu.VMEM),
-        compiler_params=pltpu.CompilerParams(vmem_limit_bytes=48 * 1024 * 1024),
+        scratch_shapes=[
+            pltpu.VMEM((heads_kv, group * rows, DH), jnp.bfloat16),
+            pltpu.VMEM((heads_kv, group * rows, 1), jnp.float32),
+            pltpu.VMEM((heads_kv, group * rows, 1), jnp.float32),
+            pltpu.VMEM((heads_kv, group * rows, DH), jnp.float32),
+        ],
+        compiler_params=pltpu.CompilerParams(vmem_limit_bytes=56 * 1024 * 1024),
     )(flags, queries, *pieces)
 
 

time: 432 us -> 324 us (0.75)
  Pallas kernels: 210 us -> 97.2 us
  starting transfers between devices: 98.1 us -> 120 us
  local copies, waits for them, and re-layouts: 29.6 us -> 19.2 us
  waiting for transfers between devices: 39.6 us -> 33.6 us
    pallas_call x1, Pallas kernels: 210 us -> 97.2 us  [attend(): pl.pallas_call(attention_kernel, out_shape=jax.ShapeDtypeStruct(queries.s...]
    ppermute x21, starting transfers between devices: 88.6 us -> 111 us  [shifted(): return lax.ppermute(block, axis, route)]
    unnamed x24 -> x30, local copies, waits for them, and re-layouts: 27 us -> 16.6 us
    ppermute x21, waiting for transfers between devices: 39.5 us -> 33.6 us  [shifted(): return lax.ppermute(block, axis, route)]
  transfers between devices with their start and end apart: 22 -> 22, of which waited for: 11 -> 8; matrix products, arithmetic and copies ran while one was open for 7% -> 7% of each run, Pallas kernels for 0% -> 0%
where the time goes in v1:
time: 324 us; the launch traced here: 321 us
  starting transfers between devices  120 us (37%)
  Pallas kernels  97.2 us (30%)
  waiting for transfers between devices  33.6 us (10%)
  blocking collectives  23 us (7%)
  between operations  19.7 us (6%)
  local copies, waits for them, and re-layouts  19.2 us (6%)
  other arithmetic  6.86 us (2%)
    ppermute x21, starting transfers between devices, shifted(): return lax.ppermute(block, axis, route)  111 us
    pallas_call x1, Pallas kernels, attend(): pl.pallas_call(attention_kernel, out_shape=jax.ShapeDtypeStruct(queries.s...  97.2 us
    ppermute x21, waiting for transfers between devices, shifted(): return lax.ppermute(block, axis, route)  33.6 us
    all_to_all x1, blocking collectives, shards(): lax.all_to_all(jnp.concatenate([keys, values], axis=1).reshape(devices, r...  23 us
    unnamed x30, local copies, waits for them, and re-layouts  16.6 us
    all_to_all x1, starting transfers between devices, shards(): lax.all_to_all(queries.reshape(devices, run_rows, width_q), 'seq', split_...  8.93 us
  transfers between devices with their start and end apart: 22, of which 8 were waited for; matrix products, arithmetic and copies ran while one was open for 7% of the time, Pallas kernels for 0%

profile of v1, /device:TPU:9, one launch (start us, length us, event | category | flops | bytes accessed | tf_op | source)
XLA Modules:
  0.0 320.7 jit_solution(12304522884067183440)
XLA Ops:
  3.6 23.0 %all_to_all.10 = bf16[128,2,1024]{2,1,0:T(2,128)(2,1)S(1)} all-to-all(bf16[128,2,1024]{2,1,0:T(2,128)(2,1)S(1)} %reshape.73), channel_id=1, replica_groups=mesh['seq'=128] {'seq'}, dimensions={0} | all-to-all | bytes 1048576 | tf_op jit(solution)/shard_map/all_to_all | solution.py:122
  29.3 3.2 %collective-permute-start.1 = (bf16[128,2048]{1,0:T(8,128)(2,1)S(1)}, bf16[128,2048]{1,0:T(8,128)(2,1)S(1)}, u32[]{:S(2)}, u32[]{:S(2)}) collective-permute-start(bf16[128,2048]{1,0:T(8,128)(2,1)S(1)} %bitcast.67), channel_id=1, source_target_pairs={{1,0},{2,1},{3,2},{4,3},{5,4},{6,5},{7,6},{8,7},{9,8},{10,9},{11,1... | collective-permute-start | bytes 1572872 | tf_op jit(solution)/shard_map/ppermute | solution.py:19
  32.5 2.9 collective-permute-done.refs_1_
  35.4 4.4 %collective-permute-start.2 = (bf16[128,2048]{1,0:T(8,128)(2,1)S(1)}, bf16[128,2048]{1,0:T(8,128)(2,1)S(1)}, u32[]{:S(2)}, u32[]{:S(2)}) collective-permute-start(bf16[128,2048]{1,0:T(8,128)(2,1)S(1)} %collective-permute-done.refs_1_), channel_id=1, source_target_pairs={{0,1},{1,2},{2,3},{3,4},{4,5},{5,6},{6,7},{7,8},{8,9},{9,10},{10,1... | collective-permute-start | bytes 1572872 | tf_op jit(solution)/shard_map/ppermute | solution.py:19
  40.1 7.1 %collective-permute-start.3 = (bf16[128,2048]{1,0:T(8,128)(2,1)S(1)}, bf16[128,2048]{1,0:T(8,128)(2,1)S(1)}, u32[]{:S(2)}, u32[]{:S(2)}) collective-permute-start(bf16[128,2048]{1,0:T(8,128)(2,1)S(1)} %collective-permute-done.1.refs_2_), channel_id=1, source_target_pairs={{1,0},{2,1},{3,2},{4,3},{5,4},{6,5},{7,6},{8,7},{9,8},{10,9},{11,1... | collective-permute-start | bytes 1572872 | tf_op jit(solution)/shard_map/ppermute | solution.py:19
  47.3 3.0 collective-permute-start.4
  50.6 11.4 %collective-permute-start.5 = (bf16[128,2048]{1,0:T(8,128)(2,1)S(1)}, bf16[128,2048]{1,0:T(8,128)(2,1)}, u32[]{:S(2)}, u32[]{:S(2)}) collective-permute-start(bf16[128,2048]{1,0:T(8,128)(2,1)S(1)} %collective-permute-done.3.refs_4_), channel_id=1, source_target_pairs={{1,0},{2,1},{3,2},{4,3},{5,4},{6,5},{7,6},{8,7},{9,8},{10,9},{11,1... | collective-permute-start | bytes 1572872 | tf_op jit(solution)/shard_map/ppermute | solution.py:19
  63.9 12.8 %collective-permute-start.7 = (bf16[128,2048]{1,0:T(8,128)(2,1)}, bf16[128,2048]{1,0:T(8,128)(2,1)}, u32[]{:S(2)}, u32[]{:S(2)}) collective-permute-start(bf16[128,2048]{1,0:T(8,128)(2,1)} %collective-permute-done.5.refs_6_), channel_id=1, source_target_pairs={{1,0},{2,1},{3,2},{4,3},{5,4},{6,5},{7,6},{8,7},{9,8},{10,9},{11,1... | collective-permute-start | bytes 1572872 | tf_op jit(solution)/shard_map/ppermute | solution.py:19
  76.8 3.9 %reduce.1 = bf16[128,8192]{1,0:T(8,128)(2,1)S(1)} reduce(bf16[128,1,8192]{2,0,1:T(8,128)(2,1)} %bitcast.69, bf16[]{:T(256)} %broadcast.3), dimensions={1}, to_apply=%copy.14.reduce_sub_computation | reduce | bytes 4194306 | tf_op jit(solution)/shard_map/reshape | solution.py:120
  80.7 2.8 reshape.71
  83.5 8.9 %all-to-all-start = ((bf16[128,2,4096]{2,1,0:T(2,128)(2,1)}), bf16[128,2,4096]{2,1,0:T(2,128)(2,1)S(1)}, u32[]{:S(2)}, u32[]{:S(2)}) async-start(bf16[128,2,4096]{2,1,0:T(2,128)(2,1)} %reshape.71), calls=%async_computation | async-start | bytes 4194304 | tf_op jit(solution)/shard_map/all_to_all | solution.py:119
  92.4 3.6 %collective-permute-start.8 = (bf16[128,2048]{1,0:T(8,128)(2,1)}, bf16[128,2048]{1,0:T(8,128)(2,1)S(1)}, u32[]{:S(2)}, u32[]{:S(2)}) collective-permute-start(bf16[128,2048]{1,0:T(8,128)(2,1)} %collective-permute-done.6.refs_7_), channel_id=1, source_target_pairs={{0,1},{1,2},{2,3},{3,4},{4,5},{5,6},{6,7},{7,8},{8,9},{9,10},{10,1... | collective-permute-start | bytes 1572872 | tf_op jit(solution)/shard_map/ppermute | solution.py:19
  97.9 23.3 %collective-permute-done.8.refs_9_ = bf16[128,2048]{1,0:T(8,128)(2,1)S(1)} collective-permute-done((bf16[128,2048]{1,0:T(8,128)(2,1)}, bf16[128,2048]{1,0:T(8,128)(2,1)S(1)}, u32[]{:S(2)}, u32[]{:S(2)}) %collective-permute-start.8) | collective-permute-done | bytes 524320 | tf_op jit(solution)/shard_map/ppermute | solution.py:19
  121.2 4.3 %collective-permute-start.10 = (bf16[128,2048]{1,0:T(8,128)(2,1)S(1)}, bf16[128,2048]{1,0:T(8,128)(2,1)}, u32[]{:S(2)}, u32[]{:S(2)}) collective-permute-start(bf16[128,2048]{1,0:T(8,128)(2,1)S(1)} %collective-permute-done.8.refs_9_), channel_id=1, source_target_pairs={{0,1},{1,2},{2,3},{3,4},{4,5},{5,6},{6,7},{7,8},{8,9},{9,10},{10,1... | collective-permute-start | bytes 1572872 | tf_op jit(solution)/shard_map/ppermute | solution.py:19
  125.5 5.5 %collective-permute-start.11 = (bf16[128,2048]{1,0:T(8,128)(2,1)S(1)}, bf16[128,2048]{1,0:T(8,128)(2,1)}, u32[]{:S(2)}, u32[]{:S(2)}) collective-permute-start(bf16[128,2048]{1,0:T(8,128)(2,1)S(1)} %collective-permute-done.9.refs_10_), channel_id=1, source_target_pairs={{1,0},{2,1},{3,2},{4,3},{5,4},{6,5},{7,6},{8,7},{9,8},{10,9},{11,1... | collective-permute-start | bytes 1572872 | tf_op jit(solution)/shard_map/ppermute | solution.py:19
  131.6 4.5 %collective-permute-start.12 = (bf16[128,2048]{1,0:T(8,128)(2,1)}, bf16[128,2048]{1,0:T(8,128)(2,1)}, u32[]{:S(2)}, u32[]{:S(2)}) collective-permute-start(bf16[128,2048]{1,0:T(8,128)(2,1)} %collective-permute-done.10.refs_11_), channel_id=1, source_target_pairs={{0,1},{1,2},{2,3},{3,4},{4,5},{5,6},{6,7},{7,8},{8,9},{9,10},{10,1... | collective-permute-start | bytes 1572872 | tf_op jit(solution)/shard_map/ppermute | solution.py:19
  136.4 9.4 %collective-permute-start.13 = (bf16[128,2048]{1,0:T(8,128)(2,1)}, bf16[128,2048]{1,0:T(8,128)(2,1)}, u32[]{:S(2)}, u32[]{:S(2)}) collective-permute-start(bf16[128,2048]{1,0:T(8,128)(2,1)} %collective-permute-done.11.refs_12_), channel_id=1, source_target_pairs={{1,0},{2,1},{3,2},{4,3},{5,4},{6,5},{7,6},{8,7},{9,8},{10,9},{11,1... | collective-permute-start | bytes 1572872 | tf_op jit(solution)/shard_map/ppermute | solution.py:19
  167.0 6.8 %reshape.72 = bf16[128,1,8192]{2,1,0:T(2,128)(2,1)} reshape(bf16[128,2,4096]{2,1,0:T(2,128)(2,1)S(1)} %all-to-all-done) | data formatting | bytes 4194304
  173.8 5.8 %copy.20 = bf16[128,1,8192]{2,0,1:T(8,128)(2,1)} copy(bf16[128,1,8192]{2,1,0:T(2,128)(2,1)} %reshape.72) | data formatting | bytes 4194304
  179.6 97.2 %shard_map.68 = bf16[128,8192]{1,0:T(8,128)(2,1)} custom-call(s32[15]{0:T(128)} %stack.103.flags_ref, bf16[128,8192]{1,0:T(8,128)(2,1)} %bitcast.65, bf16[128,2048]{1,0:T(8,128)(2,1)} %bitcast.68, bf16[128,2048]{1,0:T(8,128)(2,1)} %copy-done.2, bf16[128,2048]{1,0:T(8,128)(2,1)} %copy-done.3, bf16[128,2048]{1,0:T(8,128)(2,1)} %copy-done.4, ...), custom_call_target="tpu_custom_call" | custom-call | tf_op jit(solution)/shard_map/pallas_call | solution.py:96
  277.9 1.9 collective-permute-start.14
  285.6 24.7 %collective-permute-start.18 = (f32[1,16]{1,0:T(1,128)S(1)}, f32[1,16]{1,0:T(1,128)S(1)}, u32[]{:S(2)}, u32[]{:S(2)}) collective-permute-start(f32[1,16]{1,0:T(1,128)S(1)} %get-tuple-element.18), channel_id=1, source_target_pairs={{0,5},{1,6},{2,7},{3,8},{4,9},{5,10},{6,11},{7,12},{8,13},{9,14},{... | collective-permute-start | bytes 200 | tf_op jit(solution)/shard_map/ppermute | solution.py:19
  314.3 3.4 %collective-permute-done.19 = f32[1,16]{1,0:T(1,128)S(1)} collective-permute-done((f32[1,16]{1,0:T(1,128)S(1)}, f32[1,16]{1,0:T(1,128)S(1)}, u32[]{:S(2)}, u32[]{:S(2)}) %collective-permute-start.19) | collective-permute-done | bytes 96 | tf_op jit(solution)/shard_map/ppermute | solution.py:19
  317.7 2.5 collective-permute-done.20
  (69 shorter events, 24.8 us)
Async XLA Ops:
  0.6 276.2 %copy-start = (bf16[8192,16]{0,1:T(8,128)(2,1)S(1)}, bf16[8192,16]{0,1:T(8,128)(2,1)}, u32[]{:S(2)}) copy-start(bf16[8192,16]{0,1:T(8,128)(2,1)} %param.9) | copy-start | bytes 786436
  27.4 8.0 %collective-permute-start = (bf16[128,2048]{1,0:T(8,128)(2,1)S(1)}, bf16[128,2048]{1,0:T(8,128)(2,1)S(1)}, u32[]{:S(2)}, u32[]{:S(2)}) collective-permute-start(bf16[128,2048]{1,0:T(8,128)(2,1)S(1)} %bitcast.66), channel_id=1, source_target_pairs={{0,1},{1,2},{2,3},{3,4},{4,5},{5,6},{6,7},{7,8},{8,9},{9,10},{10,1... | collective-permute-start | bytes 1572872 | tf_op jit(solution)/shard_map/ppermute | solution.py:19
  29.3 10.8 %collective-permute-start.1 = (bf16[128,2048]{1,0:T(8,128)(2,1)S(1)}, bf16[128,2048]{1,0:T(8,128)(2,1)S(1)}, u32[]{:S(2)}, u32[]{:S(2)}) collective-permute-start(bf16[128,2048]{1,0:T(8,128)(2,1)S(1)} %bitcast.67), channel_id=1, source_target_pairs={{1,0},{2,1},{3,2},{4,3},{5,4},{6,5},{7,6},{8,7},{9,8},{10,9},{11,1... | collective-permute-start | bytes 1572872 | tf_op jit(solution)/shard_map/ppermute | solution.py:19
  35.4 11.8 %collective-permute-start.2 = (bf16[128,2048]{1,0:T(8,128)(2,1)S(1)}, bf16[128,2048]{1,0:T(8,128)(2,1)S(1)}, u32[]{:S(2)}, u32[]{:S(2)}) collective-permute-start(bf16[128,2048]{1,0:T(8,128)(2,1)S(1)} %collective-permute-done.refs_1_), channel_id=1, source_target_pairs={{0,1},{1,2},{2,3},{3,4},{4,5},{5,6},{6,7},{7,8},{8,9},{9,10},{10,1... | collective-permute-start | bytes 1572872 | tf_op jit(solution)/shard_map/ppermute | solution.py:19
  40.1 10.5 %collective-permute-start.3 = (bf16[128,2048]{1,0:T(8,128)(2,1)S(1)}, bf16[128,2048]{1,0:T(8,128)(2,1)S(1)}, u32[]{:S(2)}, u32[]{:S(2)}) collective-permute-start(bf16[128,2048]{1,0:T(8,128)(2,1)S(1)} %collective-permute-done.1.refs_2_), channel_id=1, source_target_pairs={{1,0},{2,1},{3,2},{4,3},{5,4},{6,5},{7,6},{8,7},{9,8},{10,9},{11,1... | collective-permute-start | bytes 1572872 | tf_op jit(solution)/shard_map/ppermute | solution.py:19
  47.3 14.7 %collective-permute-start.4 = (bf16[128,2048]{1,0:T(8,128)(2,1)S(1)}, bf16[128,2048]{1,0:T(8,128)(2,1)}, u32[]{:S(2)}, u32[]{:S(2)}) collective-permute-start(bf16[128,2048]{1,0:T(8,128)(2,1)S(1)} %collective-permute-done.2.refs_3_), channel_id=1, source_target_pairs={{0,1},{1,2},{2,3},{3,4},{4,5},{5,6},{6,7},{7,8},{8,9},{9,10},{10,1... | collective-permute-start | bytes 1572872 | tf_op jit(solution)/shard_map/ppermute | solution.py:19
  50.6 13.3 %collective-permute-start.5 = (bf16[128,2048]{1,0:T(8,128)(2,1)S(1)}, bf16[128,2048]{1,0:T(8,128)(2,1)}, u32[]{:S(2)}, u32[]{:S(2)}) collective-permute-start(bf16[128,2048]{1,0:T(8,128)(2,1)S(1)} %collective-permute-done.3.refs_4_), channel_id=1, source_target_pairs={{1,0},{2,1},{3,2},{4,3},{5,4},{6,5},{7,6},{8,7},{9,8},{10,9},{11,1... | collective-permute-start | bytes 1572872 | tf_op jit(solution)/shard_map/ppermute | solution.py:19
  62.0 30.4 %collective-permute-start.6 = (bf16[128,2048]{1,0:T(8,128)(2,1)}, bf16[128,2048]{1,0:T(8,128)(2,1)}, u32[]{:S(2)}, u32[]{:S(2)}) collective-permute-start(bf16[128,2048]{1,0:T(8,128)(2,1)} %collective-permute-done.4.refs_5_), channel_id=1, source_target_pairs={{0,1},{1,2},{2,3},{3,4},{4,5},{5,6},{6,7},{7,8},{8,9},{9,10},{10,1... | collective-permute-start | bytes 1572872 | tf_op jit(solution)/shard_map/ppermute | solution.py:19
  63.9 32.1 %collective-permute-start.7 = (bf16[128,2048]{1,0:T(8,128)(2,1)}, bf16[128,2048]{1,0:T(8,128)(2,1)}, u32[]{:S(2)}, u32[]{:S(2)}) collective-permute-start(bf16[128,2048]{1,0:T(8,128)(2,1)} %collective-permute-done.5.refs_6_), channel_id=1, source_target_pairs={{1,0},{2,1},{3,2},{4,3},{5,4},{6,5},{7,6},{8,7},{9,8},{10,9},{11,1... | collective-permute-start | bytes 1572872 | tf_op jit(solution)/shard_map/ppermute | solution.py:19
  83.5 62.4 %copy-start.8 = (s32[32]{0:T(128)S(1)}, s32[32]{0:T(128)}, u32[]{:S(2)}) copy-start(s32[32]{0:T(128)} %param.8) | copy-start | bytes 388
  83.5 83.5 %all-to-all-start = ((bf16[128,2,4096]{2,1,0:T(2,128)(2,1)}), bf16[128,2,4096]{2,1,0:T(2,128)(2,1)S(1)}, u32[]{:S(2)}, u32[]{:S(2)}) async-start(bf16[128,2,4096]{2,1,0:T(2,128)(2,1)} %reshape.71), calls=%async_computation | async-start | bytes 4194304 | tf_op jit(solution)/shard_map/all_to_all | solution.py:119
  92.4 28.8 %collective-permute-start.8 = (bf16[128,2048]{1,0:T(8,128)(2,1)}, bf16[128,2048]{1,0:T(8,128)(2,1)S(1)}, u32[]{:S(2)}, u32[]{:S(2)}) collective-permute-start(bf16[128,2048]{1,0:T(8,128)(2,1)} %collective-permute-done.6.refs_7_), channel_id=1, source_target_pairs={{0,1},{1,2},{2,3},{3,4},{4,5},{5,6},{6,7},{7,8},{8,9},{9,10},{10,1... | collective-permute-start | bytes 1572872 | tf_op jit(solution)/shard_map/ppermute | solution.py:19
  96.0 29.5 %collective-permute-start.9 = (bf16[128,2048]{1,0:T(8,128)(2,1)}, bf16[128,2048]{1,0:T(8,128)(2,1)S(1)}, u32[]{:S(2)}, u32[]{:S(2)}) collective-permute-start(bf16[128,2048]{1,0:T(8,128)(2,1)} %collective-permute-done.7.refs_8_), channel_id=1, source_target_pairs={{1,0},{2,1},{3,2},{4,3},{5,4},{6,5},{7,6},{8,7},{9,8},{10,9},{11,1... | collective-permute-start | bytes 1572872 | tf_op jit(solution)/shard_map/ppermute | solution.py:19
  121.2 10.4 %collective-permute-start.10 = (bf16[128,2048]{1,0:T(8,128)(2,1)S(1)}, bf16[128,2048]{1,0:T(8,128)(2,1)}, u32[]{:S(2)}, u32[]{:S(2)}) collective-permute-start(bf16[128,2048]{1,0:T(8,128)(2,1)S(1)} %collective-permute-done.8.refs_9_), channel_id=1, source_target_pairs={{0,1},{1,2},{2,3},{3,4},{4,5},{5,6},{6,7},{7,8},{8,9},{9,10},{10,1... | collective-permute-start | bytes 1572872 | tf_op jit(solution)/shard_map/ppermute | solution.py:19
  125.5 10.9 %collective-permute-start.11 = (bf16[128,2048]{1,0:T(8,128)(2,1)S(1)}, bf16[128,2048]{1,0:T(8,128)(2,1)}, u32[]{:S(2)}, u32[]{:S(2)}) collective-permute-start(bf16[128,2048]{1,0:T(8,128)(2,1)S(1)} %collective-permute-done.9.refs_10_), channel_id=1, source_target_pairs={{1,0},{2,1},{3,2},{4,3},{5,4},{6,5},{7,6},{8,7},{9,8},{10,9},{11,1... | collective-permute-start | bytes 1572872 | tf_op jit(solution)/shard_map/ppermute | solution.py:19
  131.6 48.0 %collective-permute-start.12 = (bf16[128,2048]{1,0:T(8,128)(2,1)}, bf16[128,2048]{1,0:T(8,128)(2,1)}, u32[]{:S(2)}, u32[]{:S(2)}) collective-permute-start(bf16[128,2048]{1,0:T(8,128)(2,1)} %collective-permute-done.10.refs_11_), channel_id=1, source_target_pairs={{0,1},{1,2},{2,3},{3,4},{4,5},{5,6},{6,7},{7,8},{8,9},{9,10},{10,1... | collective-permute-start | bytes 1572872 | tf_op jit(solution)/shard_map/ppermute | solution.py:19
  136.4 43.2 %collective-permute-start.13 = (bf16[128,2048]{1,0:T(8,128)(2,1)}, bf16[128,2048]{1,0:T(8,128)(2,1)}, u32[]{:S(2)}, u32[]{:S(2)}) collective-permute-start(bf16[128,2048]{1,0:T(8,128)(2,1)} %collective-permute-done.11.refs_12_), channel_id=1, source_target_pairs={{1,0},{2,1},{3,2},{4,3},{5,4},{6,5},{7,6},{8,7},{9,8},{10,9},{11,1... | collective-permute-start | bytes 1572872 | tf_op jit(solution)/shard_map/ppermute | solution.py:19
  277.9 32.5 %collective-permute-start.14 = (f32[1,16]{1,0:T(1,128)S(1)}, f32[1,16]{1,0:T(1,128)S(1)}, u32[]{:S(2)}, u32[]{:S(2)}) collective-permute-start(f32[1,16]{1,0:T(1,128)S(1)} %get-tuple-element.18), channel_id=1, source_target_pairs={{0,1},{1,2},{2,3},{3,4},{4,5},{5,6},{6,7},{7,8},{8,9},{9,10},{10,1... | collective-permute-start | bytes 200 | tf_op jit(solution)/shard_map/ppermute | solution.py:19
  279.8 32.5 %collective-permute-start.15 = (f32[1,16]{1,0:T(1,128)S(1)}, f32[1,16]{1,0:T(1,128)S(1)}, u32[]{:S(2)}, u32[]{:S(2)}) collective-permute-start(f32[1,16]{1,0:T(1,128)S(1)} %get-tuple-element.18), channel_id=1, source_target_pairs={{0,2},{1,3},{2,4},{3,5},{4,6},{5,7},{6,8},{7,9},{8,10},{9,11},{10,... | collective-permute-start | bytes 200 | tf_op jit(solution)/shard_map/ppermute | solution.py:19
  281.8 32.5 %collective-permute-start.16 = (f32[1,16]{1,0:T(1,128)S(1)}, f32[1,16]{1,0:T(1,128)S(1)}, u32[]{:S(2)}, u32[]{:S(2)}) collective-permute-start(f32[1,16]{1,0:T(1,128)S(1)} %get-tuple-element.18), channel_id=1, source_target_pairs={{0,3},{1,4},{2,5},{3,6},{4,7},{5,8},{6,9},{7,10},{8,11},{9,12},{10... | collective-permute-start | bytes 200 | tf_op jit(solution)/shard_map/ppermute | solution.py:19
  283.7 30.6 %collective-permute-start.17 = (f32[1,16]{1,0:T(1,128)S(1)}, f32[1,16]{1,0:T(1,128)S(1)}, u32[]{:S(2)}, u32[]{:S(2)}) collective-permute-start(f32[1,16]{1,0:T(1,128)S(1)} %get-tuple-element.18), channel_id=1, source_target_pairs={{0,4},{1,5},{2,6},{3,7},{4,8},{5,9},{6,10},{7,11},{8,12},{9,13},{1... | collective-permute-start | bytes 200 | tf_op jit(solution)/shard_map/ppermute | solution.py:19
  285.6 28.7 %collective-permute-start.18 = (f32[1,16]{1,0:T(1,128)S(1)}, f32[1,16]{1,0:T(1,128)S(1)}, u32[]{:S(2)}, u32[]{:S(2)}) collective-permute-start(f32[1,16]{1,0:T(1,128)S(1)} %get-tuple-element.18), channel_id=1, source_target_pairs={{0,5},{1,6},{2,7},{3,8},{4,9},{5,10},{6,11},{7,12},{8,13},{9,14},{... | collective-permute-start | bytes 200 | tf_op jit(solution)/shard_map/ppermute | solution.py:19
  310.4 7.3 %collective-permute-start.19 = (f32[1,16]{1,0:T(1,128)S(1)}, f32[1,16]{1,0:T(1,128)S(1)}, u32[]{:S(2)}, u32[]{:S(2)}) collective-permute-start(f32[1,16]{1,0:T(1,128)S(1)} %get-tuple-element.18), channel_id=1, source_target_pairs={{0,6},{1,7},{2,8},{3,9},{4,10},{5,11},{6,12},{7,13},{8,14},{9,15},... | collective-permute-start | bytes 200 | tf_op jit(solution)/shard_map/ppermute | solution.py:19
  312.3 7.9 %collective-permute-start.20 = (f32[1,16]{1,0:T(1,128)S(1)}, f32[1,16]{1,0:T(1,128)S(1)}, u32[]{:S(2)}, u32[]{:S(2)}) collective-permute-start(f32[1,16]{1,0:T(1,128)S(1)} %get-tuple-element.18), channel_id=1, source_target_pairs={{0,7},{1,8},{2,9},{3,10},{4,11},{5,12},{6,13},{7,14},{8,15},{9,16}... | collective-permute-start | bytes 200 | tf_op jit(solution)/shard_map/ppermute | solution.py:19
  (7 other events, 291.9 us)

commit v2 on v1

--- a/solution.py
+++ b/solution.py
@@ -32,44 +32,45 @@
 def attention_kernel(flags_ref, q_ref, *refs):
     tiles = len(refs) - 5
     kv_refs = refs[:tiles]
-    out_ref, qs_ref, m_ref, l_ref, acc_ref = refs[tiles:]
-    heads_kv = qs_ref.shape[0]
-    rows = q_ref.shape[0]
-    group = qs_ref.shape[1] // rows
-    width_k = heads_kv * DH
+    out_ref, qt_ref, m_ref, l_ref, acc_ref = refs[tiles:]
+    heads = q_ref.shape[1] // DH
+    width_k = kv_refs[0].shape[1] // 2
+    heads_kv = width_k // DH
+    group = heads // heads_kv
     factor = DH ** (-0.5)
-    for h in range(heads_kv):
-        for g in range(group):
-            qs_ref[h, g * rows : (g + 1) * rows, :] = q_ref[:, (h * group + g) * DH : (h * group + g + 1) * DH]
+
+    def prep(j, carry):
+        col = pl.multiple_of(j * DH, DH)
+        qt_ref[j] = q_ref[:, pl.ds(col, DH)].astype(jnp.float32).T.astype(jnp.bfloat16)
+        return carry
+
+    lax.fori_loop(0, heads, prep, 0)
 
     def tile_step(kv_ref, first):
         def one_head(h, carry):
             kcol = pl.multiple_of(h * DH, DH)
             vcol = pl.multiple_of(width_k + h * DH, DH)
             k = kv_ref[:, pl.ds(kcol, DH)]
-            v = kv_ref[:, pl.ds(vcol, DH)]
-            s = (
-                lax.dot_general(
-                    qs_ref[h], k, (((1,), (1,)), ((), ())), preferred_element_type=jnp.float32
-                )
-                * factor
-            )
-            m1 = jnp.max(s, axis=1, keepdims=True)
-            p = jnp.exp(s - m1)
-            l1 = jnp.sum(p, axis=1, keepdims=True)
-            o1 = jnp.dot(p.astype(jnp.bfloat16), v, preferred_element_type=jnp.float32)
-            if first:
-                m_ref[h] = m1
-                l_ref[h] = l1
-                acc_ref[h] = o1
-            else:
-                m0 = m_ref[h]
-                mn = jnp.maximum(m0, m1)
-                a = jnp.exp(m0 - mn)
-                b = jnp.exp(m1 - mn)
-                m_ref[h] = mn
-                l_ref[h] = l_ref[h] * a + l1 * b
-                acc_ref[h] = acc_ref[h] * a + o1 * b
+            vt = kv_ref[:, pl.ds(vcol, DH)].astype(jnp.float32).T.astype(jnp.bfloat16)
+            for g in range(group):
+                j = h * group + g
+                st = jnp.dot(k, qt_ref[j], preferred_element_type=jnp.float32) * factor
+                m1 = jnp.max(st, axis=0, keepdims=True)
+                p = jnp.exp(st - m1)
+                l1 = jnp.sum(p, axis=0, keepdims=True)
+                ot = jnp.dot(vt, p.astype(jnp.bfloat16), preferred_element_type=jnp.float32)
+                if first:
+                    m_ref[j] = m1
+                    l_ref[j] = l1
+                    acc_ref[j] = ot
+                else:
+                    m0 = m_ref[j]
+                    mn = jnp.maximum(m0, m1)
+                    a = jnp.exp(m0 - mn)
+                    b = jnp.exp(m1 - mn)
+                    m_ref[j] = mn
+                    l_ref[j] = l_ref[j] * a + l1 * b
+                    acc_ref[j] = acc_ref[j] * a + ot * b
             return carry
 
         lax.fori_loop(0, heads_kv, one_head, 0)
@@ -81,18 +82,16 @@
         def _(kv_ref=kv_refs[t]):
             tile_step(kv_ref, False)
 
-    for h in range(heads_kv):
-        normed = acc_ref[h] / l_ref[h]
-        for g in range(group):
-            out_ref[:, (h * group + g) * DH : (h * group + g + 1) * DH] = normed[
-                g * rows : (g + 1) * rows
-            ].astype(out_ref.dtype)
+    def finish(j, carry):
+        col = pl.multiple_of(j * DH, DH)
+        out_ref[:, pl.ds(col, DH)] = (acc_ref[j] / l_ref[j]).T.astype(out_ref.dtype)
+        return carry
+
+    lax.fori_loop(0, heads, finish, 0)
 
 
 def attend(flags, queries, pieces):
-    rows = queries.shape[0]
-    heads_kv = pieces[0].shape[1] // (2 * DH)
-    group = queries.shape[1] // (heads_kv * DH)
+    heads = queries.shape[1] // DH
     return pl.pallas_call(
         attention_kernel,
         out_shape=jax.ShapeDtypeStruct(queries.shape, jnp.bfloat16),
@@ -100,10 +99,10 @@
         + [pl.BlockSpec(memory_space=pltpu.VMEM)] * (1 + len(pieces)),
         out_specs=pl.BlockSpec(memory_space=pltpu.VMEM),
         scratch_shapes=[
-            pltpu.VMEM((heads_kv, group * rows, DH), jnp.bfloat16),
-            pltpu.VMEM((heads_kv, group * rows, 1), jnp.float32),
-            pltpu.VMEM((heads_kv, group * rows, 1), jnp.float32),
-            pltpu.VMEM((heads_kv, group * rows, DH), jnp.float32),
+            pltpu.VMEM((heads, DH, queries.shape[0]), jnp.bfloat16),
+            pltpu.VMEM((heads, 1, queries.shape[0]), jnp.float32),
+            pltpu.VMEM((heads, 1, queries.shape[0]), jnp.float32),
+            pltpu.VMEM((heads, DH, queries.shape[0]), jnp.float32),
         ],
         compiler_params=pltpu.CompilerParams(vmem_limit_bytes=56 * 1024 * 1024),
     )(flags, queries, *pieces)

time: 324 us -> 262 us (0.81)
  the two profiles are of different devices: /device:TPU:9 before, /device:TPU:51 now
where the time goes in v2:
time: 262 us; the launch traced here: 261 us
  starting transfers between devices  121 us (46%)
  waiting for transfers between devices  43.1 us (16%)
  Pallas kernels  29.7 us (11%)
  blocking collectives  20.1 us (8%)
  between operations  19.7 us (8%)
  local copies, waits for them, and re-layouts  19.2 us (7%)
  other arithmetic  6.86 us (3%)
    ppermute x21, starting transfers between devices, shifted(): return lax.ppermute(block, axis, route)  96.5 us
    ppermute x21, waiting for transfers between devices, shifted(): return lax.ppermute(block, axis, route)  43.1 us
    pallas_call x1, Pallas kernels, attend(): pl.pallas_call(attention_kernel, out_shape=jax.ShapeDtypeStruct(queries.s...  29.7 us
    all_to_all x1, starting transfers between devices, shards(): lax.all_to_all(queries.reshape(devices, run_rows, width_q), 'seq', split_...  24.4 us
    all_to_all x1, blocking collectives, shards(): lax.all_to_all(jnp.concatenate([keys, values], axis=1).reshape(devices, r...  20.1 us
    unnamed x30, local copies, waits for them, and re-layouts  16.6 us
  transfers between devices with their start and end apart: 22, of which 6 were waited for; matrix products, arithmetic and copies ran while one was open for 8% of the time, Pallas kernels for 0%

profile of v2, /device:TPU:51, one launch (start us, length us, event | category | flops | bytes accessed | tf_op | source)
XLA Modules:
  0.0 260.6 jit_solution(14447712084397582954)
XLA Ops:
  3.6 20.1 %all_to_all.10 = bf16[128,2,1024]{2,1,0:T(2,128)(2,1)S(1)} all-to-all(bf16[128,2,1024]{2,1,0:T(2,128)(2,1)S(1)} %reshape.73), channel_id=1, replica_groups=mesh['seq'=128] {'seq'}, dimensions={0} | all-to-all | bytes 1048576 | tf_op jit(solution)/shard_map/all_to_all | solution.py:121
  24.5 2.9 %collective-permute-start = (bf16[128,2048]{1,0:T(8,128)(2,1)S(1)}, bf16[128,2048]{1,0:T(8,128)(2,1)S(1)}, u32[]{:S(2)}, u32[]{:S(2)}) collective-permute-start(bf16[128,2048]{1,0:T(8,128)(2,1)S(1)} %bitcast.66), channel_id=1, source_target_pairs={{0,1},{1,2},{2,3},{3,4},{4,5},{5,6},{6,7},{7,8},{8,9},{9,10},{10,1... | collective-permute-start | bytes 1572872 | tf_op jit(solution)/shard_map/ppermute | solution.py:19
  29.4 4.2 %collective-permute-done.refs_1_ = bf16[128,2048]{1,0:T(8,128)(2,1)S(1)} collective-permute-done((bf16[128,2048]{1,0:T(8,128)(2,1)S(1)}, bf16[128,2048]{1,0:T(8,128)(2,1)S(1)}, u32[]{:S(2)}, u32[]{:S(2)}) %collective-permute-start) | collective-permute-done | bytes 524320 | tf_op jit(solution)/shard_map/ppermute | solution.py:19
  33.6 4.4 %collective-permute-start.2 = (bf16[128,2048]{1,0:T(8,128)(2,1)S(1)}, bf16[128,2048]{1,0:T(8,128)(2,1)S(1)}, u32[]{:S(2)}, u32[]{:S(2)}) collective-permute-start(bf16[128,2048]{1,0:T(8,128)(2,1)S(1)} %collective-permute-done.refs_1_), channel_id=1, source_target_pairs={{0,1},{1,2},{2,3},{3,4},{4,5},{5,6},{6,7},{7,8},{8,9},{9,10},{10,1... | collective-permute-start | bytes 1572872 | tf_op jit(solution)/shard_map/ppermute | solution.py:19
  39.9 4.2 %collective-permute-done.2.refs_3_ = bf16[128,2048]{1,0:T(8,128)(2,1)S(1)} collective-permute-done((bf16[128,2048]{1,0:T(8,128)(2,1)S(1)}, bf16[128,2048]{1,0:T(8,128)(2,1)S(1)}, u32[]{:S(2)}, u32[]{:S(2)}) %collective-permute-start.2) | collective-permute-done | bytes 524320 | tf_op jit(solution)/shard_map/ppermute | solution.py:19
  44.0 4.4 %collective-permute-start.4 = (bf16[128,2048]{1,0:T(8,128)(2,1)S(1)}, bf16[128,2048]{1,0:T(8,128)(2,1)}, u32[]{:S(2)}, u32[]{:S(2)}) collective-permute-start(bf16[128,2048]{1,0:T(8,128)(2,1)S(1)} %collective-permute-done.2.refs_3_), channel_id=1, source_target_pairs={{0,1},{1,2},{2,3},{3,4},{4,5},{5,6},{6,7},{7,8},{8,9},{9,10},{10,1... | collective-permute-start | bytes 1572872 | tf_op jit(solution)/shard_map/ppermute | solution.py:19
  50.4 4.2 %collective-permute-done.4.refs_5_ = bf16[128,2048]{1,0:T(8,128)(2,1)} collective-permute-done((bf16[128,2048]{1,0:T(8,128)(2,1)S(1)}, bf16[128,2048]{1,0:T(8,128)(2,1)}, u32[]{:S(2)}, u32[]{:S(2)}) %collective-permute-start.4) | collective-permute-done | bytes 524320 | tf_op jit(solution)/shard_map/ppermute | solution.py:19
  54.5 4.5 %collective-permute-start.6 = (bf16[128,2048]{1,0:T(8,128)(2,1)}, bf16[128,2048]{1,0:T(8,128)(2,1)}, u32[]{:S(2)}, u32[]{:S(2)}) collective-permute-start(bf16[128,2048]{1,0:T(8,128)(2,1)} %collective-permute-done.4.refs_5_), channel_id=1, source_target_pairs={{0,1},{1,2},{2,3},{3,4},{4,5},{5,6},{6,7},{7,8},{8,9},{9,10},{10,1... | collective-permute-start | bytes 1572872 | tf_op jit(solution)/shard_map/ppermute | solution.py:19
  61.0 3.9 %reduce.1 = bf16[128,8192]{1,0:T(8,128)(2,1)S(1)} reduce(bf16[128,1,8192]{2,0,1:T(8,128)(2,1)} %bitcast.69, bf16[]{:T(256)} %broadcast.3), dimensions={1}, to_apply=%copy.14.reduce_sub_computation | reduce | bytes 4194306 | tf_op jit(solution)/shard_map/reshape | solution.py:119
  67.7 24.4 %all-to-all-start = ((bf16[128,2,4096]{2,1,0:T(2,128)(2,1)}), bf16[128,2,4096]{2,1,0:T(2,128)(2,1)S(1)}, u32[]{:S(2)}, u32[]{:S(2)}) async-start(bf16[128,2,4096]{2,1,0:T(2,128)(2,1)} %reshape.71), calls=%async_computation | async-start | bytes 4194304 | tf_op jit(solution)/shard_map/all_to_all | solution.py:118
  92.1 3.6 %collective-permute-start.8 = (bf16[128,2048]{1,0:T(8,128)(2,1)}, bf16[128,2048]{1,0:T(8,128)(2,1)S(1)}, u32[]{:S(2)}, u32[]{:S(2)}) collective-permute-start(bf16[128,2048]{1,0:T(8,128)(2,1)} %collective-permute-done.6.refs_7_), channel_id=1, source_target_pairs={{0,1},{1,2},{2,3},{3,4},{4,5},{5,6},{6,7},{7,8},{8,9},{9,10},{10,1... | collective-permute-start | bytes 1572872 | tf_op jit(solution)/shard_map/ppermute | solution.py:19
  97.7 22.6 %collective-permute-done.8.refs_9_ = bf16[128,2048]{1,0:T(8,128)(2,1)S(1)} collective-permute-done((bf16[128,2048]{1,0:T(8,128)(2,1)}, bf16[128,2048]{1,0:T(8,128)(2,1)S(1)}, u32[]{:S(2)}, u32[]{:S(2)}) %collective-permute-start.8) | collective-permute-done | bytes 524320 | tf_op jit(solution)/shard_map/ppermute | solution.py:19
  120.3 4.3 %collective-permute-start.10 = (bf16[128,2048]{1,0:T(8,128)(2,1)S(1)}, bf16[128,2048]{1,0:T(8,128)(2,1)}, u32[]{:S(2)}, u32[]{:S(2)}) collective-permute-start(bf16[128,2048]{1,0:T(8,128)(2,1)S(1)} %collective-permute-done.8.refs_9_), channel_id=1, source_target_pairs={{0,1},{1,2},{2,3},{3,4},{4,5},{5,6},{6,7},{7,8},{8,9},{9,10},{10,1... | collective-permute-start | bytes 1572872 | tf_op jit(solution)/shard_map/ppermute | solution.py:19
  126.5 4.2 %collective-permute-done.10.refs_11_ = bf16[128,2048]{1,0:T(8,128)(2,1)} collective-permute-done((bf16[128,2048]{1,0:T(8,128)(2,1)S(1)}, bf16[128,2048]{1,0:T(8,128)(2,1)}, u32[]{:S(2)}, u32[]{:S(2)}) %collective-permute-start.10) | collective-permute-done | bytes 524320 | tf_op jit(solution)/shard_map/ppermute | solution.py:19
  130.7 4.5 %collective-permute-start.12 = (bf16[128,2048]{1,0:T(8,128)(2,1)}, bf16[128,2048]{1,0:T(8,128)(2,1)}, u32[]{:S(2)}, u32[]{:S(2)}) collective-permute-start(bf16[128,2048]{1,0:T(8,128)(2,1)} %collective-permute-done.10.refs_11_), channel_id=1, source_target_pairs={{0,1},{1,2},{2,3},{3,4},{4,5},{5,6},{6,7},{7,8},{8,9},{9,10},{10,1... | collective-permute-start | bytes 1572872 | tf_op jit(solution)/shard_map/ppermute | solution.py:19
  158.2 6.8 %reshape.72 = bf16[128,1,8192]{2,1,0:T(2,128)(2,1)} reshape(bf16[128,2,4096]{2,1,0:T(2,128)(2,1)S(1)} %all-to-all-done) | data formatting | bytes 4194304
  165.0 5.8 %copy.20 = bf16[128,1,8192]{2,0,1:T(8,128)(2,1)} copy(bf16[128,1,8192]{2,1,0:T(2,128)(2,1)} %reshape.72) | data formatting | bytes 4194304
  170.9 29.7 %shard_map.68 = bf16[128,8192]{1,0:T(8,128)(2,1)} custom-call(s32[15]{0:T(128)} %stack.103.flags_ref, bf16[128,8192]{1,0:T(8,128)(2,1)} %bitcast.65, bf16[128,2048]{1,0:T(8,128)(2,1)} %bitcast.68, bf16[128,2048]{1,0:T(8,128)(2,1)} %copy-done.2, bf16[128,2048]{1,0:T(8,128)(2,1)} %copy-done.3, bf16[128,2048]{1,0:T(8,128)(2,1)} %copy-done.4, ...), custom_call_target="tpu_custom_call" | custom-call | tf_op jit(solution)/shard_map/pallas_call | solution.py:95
  201.7 3.7 %collective-permute-start.14 = (f32[1,16]{1,0:T(1,128)S(1)}, f32[1,16]{1,0:T(1,128)S(1)}, u32[]{:S(2)}, u32[]{:S(2)}) collective-permute-start(f32[1,16]{1,0:T(1,128)S(1)} %get-tuple-element.18), channel_id=1, source_target_pairs={{0,1},{1,2},{2,3},{3,4},{4,5},{5,6},{6,7},{7,8},{8,9},{9,10},{10,1... | collective-permute-start | bytes 200 | tf_op jit(solution)/shard_map/ppermute | solution.py:19
  205.3 18.1 %collective-permute-start.15 = (f32[1,16]{1,0:T(1,128)S(1)}, f32[1,16]{1,0:T(1,128)S(1)}, u32[]{:S(2)}, u32[]{:S(2)}) collective-permute-start(f32[1,16]{1,0:T(1,128)S(1)} %get-tuple-element.18), channel_id=1, source_target_pairs={{0,2},{1,3},{2,4},{3,5},{4,6},{5,7},{6,8},{7,9},{8,10},{9,11},{10,... | collective-permute-start | bytes 200 | tf_op jit(solution)/shard_map/ppermute | solution.py:19
  223.4 10.1 %collective-permute-start.16 = (f32[1,16]{1,0:T(1,128)S(1)}, f32[1,16]{1,0:T(1,128)S(1)}, u32[]{:S(2)}, u32[]{:S(2)}) collective-permute-start(f32[1,16]{1,0:T(1,128)S(1)} %get-tuple-element.18), channel_id=1, source_target_pairs={{0,3},{1,4},{2,5},{3,6},{4,7},{5,8},{6,9},{7,10},{8,11},{9,12},{10... | collective-permute-start | bytes 200 | tf_op jit(solution)/shard_map/ppermute | solution.py:19
  235.4 8.2 %collective-permute-start.18 = (f32[1,16]{1,0:T(1,128)S(1)}, f32[1,16]{1,0:T(1,128)S(1)}, u32[]{:S(2)}, u32[]{:S(2)}) collective-permute-start(f32[1,16]{1,0:T(1,128)S(1)} %get-tuple-element.18), channel_id=1, source_target_pairs={{0,5},{1,6},{2,7},{3,8},{4,9},{5,10},{6,11},{7,12},{8,13},{9,14},{... | collective-permute-start | bytes 200 | tf_op jit(solution)/shard_map/ppermute | solution.py:19
  243.6 10.7 %collective-permute-start.19 = (f32[1,16]{1,0:T(1,128)S(1)}, f32[1,16]{1,0:T(1,128)S(1)}, u32[]{:S(2)}, u32[]{:S(2)}) collective-permute-start(f32[1,16]{1,0:T(1,128)S(1)} %get-tuple-element.18), channel_id=1, source_target_pairs={{0,6},{1,7},{2,8},{3,9},{4,10},{5,11},{6,12},{7,13},{8,14},{9,15},... | collective-permute-start | bytes 200 | tf_op jit(solution)/shard_map/ppermute | solution.py:19
  256.3 3.8 %collective-permute-done.20 = f32[1,16]{1,0:T(1,128)S(1)} collective-permute-done((f32[1,16]{1,0:T(1,128)S(1)}, f32[1,16]{1,0:T(1,128)S(1)}, u32[]{:S(2)}, u32[]{:S(2)}) %collective-permute-start.20) | collective-permute-done | bytes 96 | tf_op jit(solution)/shard_map/ppermute | solution.py:19
  (69 shorter events, 28.0 us)
Async XLA Ops:
  0.6 199.9 %copy-start = (bf16[8192,16]{0,1:T(8,128)(2,1)S(1)}, bf16[8192,16]{0,1:T(8,128)(2,1)}, u32[]{:S(2)}) copy-start(bf16[8192,16]{0,1:T(8,128)(2,1)} %param.9) | copy-start | bytes 786436
  24.5 9.1 %collective-permute-start = (bf16[128,2048]{1,0:T(8,128)(2,1)S(1)}, bf16[128,2048]{1,0:T(8,128)(2,1)S(1)}, u32[]{:S(2)}, u32[]{:S(2)}) collective-permute-start(bf16[128,2048]{1,0:T(8,128)(2,1)S(1)} %bitcast.66), channel_id=1, source_target_pairs={{0,1},{1,2},{2,3},{3,4},{4,5},{5,6},{6,7},{7,8},{8,9},{9,10},{10,1... | collective-permute-start | bytes 1572872 | tf_op jit(solution)/shard_map/ppermute | solution.py:19
  27.4 10.5 %collective-permute-start.1 = (bf16[128,2048]{1,0:T(8,128)(2,1)S(1)}, bf16[128,2048]{1,0:T(8,128)(2,1)S(1)}, u32[]{:S(2)}, u32[]{:S(2)}) collective-permute-start(bf16[128,2048]{1,0:T(8,128)(2,1)S(1)} %bitcast.67), channel_id=1, source_target_pairs={{1,0},{2,1},{3,2},{4,3},{5,4},{6,5},{7,6},{8,7},{9,8},{10,9},{11,1... | collective-permute-start | bytes 1572872 | tf_op jit(solution)/shard_map/ppermute | solution.py:19
  33.6 10.5 %collective-permute-start.2 = (bf16[128,2048]{1,0:T(8,128)(2,1)S(1)}, bf16[128,2048]{1,0:T(8,128)(2,1)S(1)}, u32[]{:S(2)}, u32[]{:S(2)}) collective-permute-start(bf16[128,2048]{1,0:T(8,128)(2,1)S(1)} %collective-permute-done.refs_1_), channel_id=1, source_target_pairs={{0,1},{1,2},{2,3},{3,4},{4,5},{5,6},{6,7},{7,8},{8,9},{9,10},{10,1... | collective-permute-start | bytes 1572872 | tf_op jit(solution)/shard_map/ppermute | solution.py:19
  38.0 10.5 %collective-permute-start.3 = (bf16[128,2048]{1,0:T(8,128)(2,1)S(1)}, bf16[128,2048]{1,0:T(8,128)(2,1)S(1)}, u32[]{:S(2)}, u32[]{:S(2)}) collective-permute-start(bf16[128,2048]{1,0:T(8,128)(2,1)S(1)} %collective-permute-done.1.refs_2_), channel_id=1, source_target_pairs={{1,0},{2,1},{3,2},{4,3},{5,4},{6,5},{7,6},{8,7},{9,8},{10,9},{11,1... | collective-permute-start | bytes 1572872 | tf_op jit(solution)/shard_map/ppermute | solution.py:19
  44.0 10.5 %collective-permute-start.4 = (bf16[128,2048]{1,0:T(8,128)(2,1)S(1)}, bf16[128,2048]{1,0:T(8,128)(2,1)}, u32[]{:S(2)}, u32[]{:S(2)}) collective-permute-start(bf16[128,2048]{1,0:T(8,128)(2,1)S(1)} %collective-permute-done.2.refs_3_), channel_id=1, source_target_pairs={{0,1},{1,2},{2,3},{3,4},{4,5},{5,6},{6,7},{7,8},{8,9},{9,10},{10,1... | collective-permute-start | bytes 1572872 | tf_op jit(solution)/shard_map/ppermute | solution.py:19
  48.5 10.6 %collective-permute-start.5 = (bf16[128,2048]{1,0:T(8,128)(2,1)S(1)}, bf16[128,2048]{1,0:T(8,128)(2,1)}, u32[]{:S(2)}, u32[]{:S(2)}) collective-permute-start(bf16[128,2048]{1,0:T(8,128)(2,1)S(1)} %collective-permute-done.3.refs_4_), channel_id=1, source_target_pairs={{1,0},{2,1},{3,2},{4,3},{5,4},{6,5},{7,6},{8,7},{9,8},{10,9},{11,1... | collective-permute-start | bytes 1572872 | tf_op jit(solution)/shard_map/ppermute | solution.py:19
  54.5 37.6 %collective-permute-start.6 = (bf16[128,2048]{1,0:T(8,128)(2,1)}, bf16[128,2048]{1,0:T(8,128)(2,1)}, u32[]{:S(2)}, u32[]{:S(2)}) collective-permute-start(bf16[128,2048]{1,0:T(8,128)(2,1)} %collective-permute-done.4.refs_5_), channel_id=1, source_target_pairs={{0,1},{1,2},{2,3},{3,4},{4,5},{5,6},{6,7},{7,8},{8,9},{9,10},{10,1... | collective-permute-start | bytes 1572872 | tf_op jit(solution)/shard_map/ppermute | solution.py:19
  59.1 36.7 %collective-permute-start.7 = (bf16[128,2048]{1,0:T(8,128)(2,1)}, bf16[128,2048]{1,0:T(8,128)(2,1)}, u32[]{:S(2)}, u32[]{:S(2)}) collective-permute-start(bf16[128,2048]{1,0:T(8,128)(2,1)} %collective-permute-done.5.refs_6_), channel_id=1, source_target_pairs={{1,0},{2,1},{3,2},{4,3},{5,4},{6,5},{7,6},{8,7},{9,8},{10,9},{11,1... | collective-permute-start | bytes 1572872 | tf_op jit(solution)/shard_map/ppermute | solution.py:19
  67.7 69.5 %copy-start.8 = (s32[32]{0:T(128)S(1)}, s32[32]{0:T(128)}, u32[]{:S(2)}) copy-start(s32[32]{0:T(128)} %param.8) | copy-start | bytes 388
  67.7 90.6 %all-to-all-start = ((bf16[128,2,4096]{2,1,0:T(2,128)(2,1)}), bf16[128,2,4096]{2,1,0:T(2,128)(2,1)S(1)}, u32[]{:S(2)}, u32[]{:S(2)}) async-start(bf16[128,2,4096]{2,1,0:T(2,128)(2,1)} %reshape.71), calls=%async_computation | async-start | bytes 4194304 | tf_op jit(solution)/shard_map/all_to_all | solution.py:118
  92.1 28.1 %collective-permute-start.8 = (bf16[128,2048]{1,0:T(8,128)(2,1)}, bf16[128,2048]{1,0:T(8,128)(2,1)S(1)}, u32[]{:S(2)}, u32[]{:S(2)}) collective-permute-start(bf16[128,2048]{1,0:T(8,128)(2,1)} %collective-permute-done.6.refs_7_), channel_id=1, source_target_pairs={{0,1},{1,2},{2,3},{3,4},{4,5},{5,6},{6,7},{7,8},{8,9},{9,10},{10,1... | collective-permute-start | bytes 1572872 | tf_op jit(solution)/shard_map/ppermute | solution.py:19
  95.8 28.8 %collective-permute-start.9 = (bf16[128,2048]{1,0:T(8,128)(2,1)}, bf16[128,2048]{1,0:T(8,128)(2,1)S(1)}, u32[]{:S(2)}, u32[]{:S(2)}) collective-permute-start(bf16[128,2048]{1,0:T(8,128)(2,1)} %collective-permute-done.7.refs_8_), channel_id=1, source_target_pairs={{1,0},{2,1},{3,2},{4,3},{5,4},{6,5},{7,6},{8,7},{9,8},{10,9},{11,1... | collective-permute-start | bytes 1572872 | tf_op jit(solution)/shard_map/ppermute | solution.py:19
  120.3 10.4 %collective-permute-start.10 = (bf16[128,2048]{1,0:T(8,128)(2,1)S(1)}, bf16[128,2048]{1,0:T(8,128)(2,1)}, u32[]{:S(2)}, u32[]{:S(2)}) collective-permute-start(bf16[128,2048]{1,0:T(8,128)(2,1)S(1)} %collective-permute-done.8.refs_9_), channel_id=1, source_target_pairs={{0,1},{1,2},{2,3},{3,4},{4,5},{5,6},{6,7},{7,8},{8,9},{9,10},{10,1... | collective-permute-start | bytes 1572872 | tf_op jit(solution)/shard_map/ppermute | solution.py:19
  124.6 10.6 %collective-permute-start.11 = (bf16[128,2048]{1,0:T(8,128)(2,1)S(1)}, bf16[128,2048]{1,0:T(8,128)(2,1)}, u32[]{:S(2)}, u32[]{:S(2)}) collective-permute-start(bf16[128,2048]{1,0:T(8,128)(2,1)S(1)} %collective-permute-done.9.refs_10_), channel_id=1, source_target_pairs={{1,0},{2,1},{3,2},{4,3},{5,4},{6,5},{7,6},{8,7},{9,8},{10,9},{11,1... | collective-permute-start | bytes 1572872 | tf_op jit(solution)/shard_map/ppermute | solution.py:19
  130.7 40.2 %collective-permute-start.12 = (bf16[128,2048]{1,0:T(8,128)(2,1)}, bf16[128,2048]{1,0:T(8,128)(2,1)}, u32[]{:S(2)}, u32[]{:S(2)}) collective-permute-start(bf16[128,2048]{1,0:T(8,128)(2,1)} %collective-permute-done.10.refs_11_), channel_id=1, source_target_pairs={{0,1},{1,2},{2,3},{3,4},{4,5},{5,6},{6,7},{7,8},{8,9},{9,10},{10,1... | collective-permute-start | bytes 1572872 | tf_op jit(solution)/shard_map/ppermute | solution.py:19
  135.2 35.7 %collective-permute-start.13 = (bf16[128,2048]{1,0:T(8,128)(2,1)}, bf16[128,2048]{1,0:T(8,128)(2,1)}, u32[]{:S(2)}, u32[]{:S(2)}) collective-permute-start(bf16[128,2048]{1,0:T(8,128)(2,1)} %collective-permute-done.11.refs_12_), channel_id=1, source_target_pairs={{1,0},{2,1},{3,2},{4,3},{5,4},{6,5},{7,6},{8,7},{9,8},{10,9},{11,1... | collective-permute-start | bytes 1572872 | tf_op jit(solution)/shard_map/ppermute | solution.py:19
  201.7 41.9 %collective-permute-start.14 = (f32[1,16]{1,0:T(1,128)S(1)}, f32[1,16]{1,0:T(1,128)S(1)}, u32[]{:S(2)}, u32[]{:S(2)}) collective-permute-start(f32[1,16]{1,0:T(1,128)S(1)} %get-tuple-element.18), channel_id=1, source_target_pairs={{0,1},{1,2},{2,3},{3,4},{4,5},{5,6},{6,7},{7,8},{8,9},{9,10},{10,1... | collective-permute-start | bytes 200 | tf_op jit(solution)/shard_map/ppermute | solution.py:19
  205.3 49.0 %collective-permute-start.15 = (f32[1,16]{1,0:T(1,128)S(1)}, f32[1,16]{1,0:T(1,128)S(1)}, u32[]{:S(2)}, u32[]{:S(2)}) collective-permute-start(f32[1,16]{1,0:T(1,128)S(1)} %get-tuple-element.18), channel_id=1, source_target_pairs={{0,2},{1,3},{2,4},{3,5},{4,6},{5,7},{6,8},{7,9},{8,10},{9,11},{10,... | collective-permute-start | bytes 200 | tf_op jit(solution)/shard_map/ppermute | solution.py:19
  223.4 32.8 %collective-permute-start.16 = (f32[1,16]{1,0:T(1,128)S(1)}, f32[1,16]{1,0:T(1,128)S(1)}, u32[]{:S(2)}, u32[]{:S(2)}) collective-permute-start(f32[1,16]{1,0:T(1,128)S(1)} %get-tuple-element.18), channel_id=1, source_target_pairs={{0,3},{1,4},{2,5},{3,6},{4,7},{5,8},{6,9},{7,10},{8,11},{9,12},{10... | collective-permute-start | bytes 200 | tf_op jit(solution)/shard_map/ppermute | solution.py:19
  233.5 22.8 %collective-permute-start.17 = (f32[1,16]{1,0:T(1,128)S(1)}, f32[1,16]{1,0:T(1,128)S(1)}, u32[]{:S(2)}, u32[]{:S(2)}) collective-permute-start(f32[1,16]{1,0:T(1,128)S(1)} %get-tuple-element.18), channel_id=1, source_target_pairs={{0,4},{1,5},{2,6},{3,7},{4,8},{5,9},{6,10},{7,11},{8,12},{9,13},{1... | collective-permute-start | bytes 200 | tf_op jit(solution)/shard_map/ppermute | solution.py:19
  235.4 20.9 %collective-permute-start.18 = (f32[1,16]{1,0:T(1,128)S(1)}, f32[1,16]{1,0:T(1,128)S(1)}, u32[]{:S(2)}, u32[]{:S(2)}) collective-permute-start(f32[1,16]{1,0:T(1,128)S(1)} %get-tuple-element.18), channel_id=1, source_target_pairs={{0,5},{1,6},{2,7},{3,8},{4,9},{5,10},{6,11},{7,12},{8,13},{9,14},{... | collective-permute-start | bytes 200 | tf_op jit(solution)/shard_map/ppermute | solution.py:19
  243.6 12.7 %collective-permute-start.19 = (f32[1,16]{1,0:T(1,128)S(1)}, f32[1,16]{1,0:T(1,128)S(1)}, u32[]{:S(2)}, u32[]{:S(2)}) collective-permute-start(f32[1,16]{1,0:T(1,128)S(1)} %get-tuple-element.18), channel_id=1, source_target_pairs={{0,6},{1,7},{2,8},{3,9},{4,10},{5,11},{6,12},{7,13},{8,14},{9,15},... | collective-permute-start | bytes 200 | tf_op jit(solution)/shard_map/ppermute | solution.py:19
  254.3 5.8 %collective-permute-start.20 = (f32[1,16]{1,0:T(1,128)S(1)}, f32[1,16]{1,0:T(1,128)S(1)}, u32[]{:S(2)}, u32[]{:S(2)}) collective-permute-start(f32[1,16]{1,0:T(1,128)S(1)} %get-tuple-element.18), channel_id=1, source_target_pairs={{0,7},{1,8},{2,9},{3,10},{4,11},{5,12},{6,13},{7,14},{8,15},{9,16}... | collective-permute-start | bytes 200 | tf_op jit(solution)/shard_map/ppermute | solution.py:19
  (7 other events, 209.6 us)

commit v3 on v2

v3 whole, which is shorter than its diff:
```python
import jax
import jax.numpy as jnp
from jax import lax
from jax.sharding import PartitionSpec as P
from jax.experimental import pallas as pl
from jax.experimental.pallas import tpu as pltpu

DH = 128
BLK = 128
MAXB = 8


def shifted(block, axis, distance):
    count = lax.axis_size(axis)
    if distance > 0:
        route = [(i - distance, i) for i in range(distance, count)]
    else:
        route = [(i - distance, i) for i in range(0, count + distance)]
    return lax.ppermute(block, axis, route)


def block_docs(lengths, block_count):
    doc_ends = jnp.cumsum(lengths, dtype=jnp.int32)
    doc_firsts = doc_ends - lengths
    blocks = jnp.arange(block_count, dtype=jnp.int32)
    owner_doc = jnp.sum((doc_ends[None, :] <= blocks[:, None]).astype(jnp.int32), axis=1)
    matches = owner_doc[:, None] == jnp.arange(lengths.shape[0], dtype=jnp.int32)[None, :]
    first_block = jnp.sum(jnp.where(matches, doc_firsts[None, :], 0), axis=1)
    return (owner_doc, first_block)


def attention_kernel(flags_ref, q_ref, q0t_ref, *refs):
    tiles = len(refs) - 9
    kv_refs = refs[:tiles]
    out_ref, out0_ref, qt_ref, m_ref, l_ref, acc_ref, m0_ref, l0_ref, acc0_ref = refs[tiles:]
    heads = q_ref.shape[0]
    rows = q_ref.shape[1]
    width_k = kv_refs[0].shape[1] // 2
    heads_kv = width_k // DH
    group = heads // heads_kv
    factor = DH ** (-0.5)

    def prep(j, carry):
        qt_ref[j] = q_ref[j].astype(jnp.float32).T.astype(jnp.bfloat16)
        return carry

    lax.fori_loop(0, heads, prep, 0)

    def merge(first, ms, ls, accs, j, m1, l1, o1):
        if first:
            ms[j] = m1
            ls[j] = l1
            accs[j] = o1
        else:
            m0 = ms[j]
            mn = jnp.maximum(m0, m1)
            a = jnp.exp(m0 - mn)
            b = jnp.exp(m1 - mn)
            ms[j] = mn
            ls[j] = ls[j] * a + l1 * b
            accs[j] = accs[j] * a + o1 * b

    def scored(k, vt, qt):
        st = jnp.dot(k, qt, preferred_element_type=jnp.float32) * factor
        m1 = jnp.max(st, axis=0, keepdims=True)
        p = jnp.exp(st - m1)
        l1 = jnp.sum(p, axis=0, keepdims=True)
        ot = jnp.dot(vt, p.astype(jnp.bfloat16), preferred_element_type=jnp.float32)
        return m1, l1, ot

    def tile_step(kv_ref, first):
        def one_head(h, carry):
            kcol = pl.multiple_of(h * DH, DH)
            vcol = pl.multiple_of(width_k + h * DH, DH)
            k = kv_ref[0:rows, pl.ds(kcol, DH)]
            vt = kv_ref[0:rows, pl.ds(vcol, DH)].astype(jnp.float32).T.astype(jnp.bfloat16)
            for g in range(group):
                j = h * group + g
                merge(first, m_ref, l_ref, acc_ref, j, *scored(k, vt, qt_ref[j]))
            merge(first, m0_ref, l0_ref, acc0_ref, h, *scored(k, vt, q0t_ref[h]))
            return carry

        lax.fori_loop(0, heads_kv, one_head, 0)

    tile_step(kv_refs[0], True)
    for t in range(1, tiles):

        @pl.when(flags_ref[t] > 0)
        def _(kv_ref=kv_refs[t]):
            tile_step(kv_ref, False)

    def finish(j, carry):
        col = pl.multiple_of(j * DH, DH)
        out_ref[:, pl.ds(col, DH)] = (acc_ref[j] / l_ref[j]).T.astype(out_ref.dtype)
        return carry

    lax.fori_loop(0, heads, finish, 0)
    for h in range(heads_kv):
        out0_ref[h] = acc0_ref[h] / l0_ref[h]


def attend(flags, q_heads, q0t, pieces):
    heads, rows, _ = q_heads.shape
    heads_kv = q0t.shape[0]
    width = q0t.shape[2]
    return pl.pallas_call(
        attention_kernel,
        out_shape=(
            jax.ShapeDtypeStruct((rows, heads * DH), jnp.bfloat16),
            jax.ShapeDtypeStruct((heads_kv, DH, width), jnp.float32),
        ),
        in_specs=[pl.BlockSpec(memory_space=pltpu.SMEM)]
        + [pl.BlockSpec(memory_space=pltpu.VMEM)] * (2 + len(pieces)),
        out_specs=(pl.BlockSpec(memory_space=pltpu.VMEM), pl.BlockSpec(memory_space=pltpu.VMEM)),
        scratch_shapes=[
            pltpu.VMEM((heads, DH, rows), jnp.bfloat16),
            pltpu.VMEM((heads, 1, rows), jnp.float32),
            pltpu.VMEM((heads, 1, rows), jnp.float32),
            pltpu.VMEM((heads, DH, rows), jnp.float32),
            pltpu.VMEM((heads_kv, 1, width), jnp.float32),
            pltpu.VMEM((heads_kv, 1, width), jnp.float32),
            pltpu.VMEM((heads_kv, DH, width), jnp.float32),
        ],
        compiler_params=pltpu.CompilerParams(vmem_limit_bytes=56 * 1024 * 1024),
    )(flags, q_heads, q0t, *pieces)


def shards(queries, keys, values, lengths, class_weight):
    devices = lax.axis_size("seq")
    myself = lax.axis_index("seq")
    row_count = queries.shape[0]
    width_q = queries.shape[1]
    width_k = keys.shape[1]
    heads = width_q // DH
    heads_kv = width_k // DH
    group = heads // heads_kv
    arrived_q = lax.all_to_all(
        queries.reshape(devices, heads, DH), "seq", split_axis=0, concat_axis=0, tiled=True
    )
    arrived_kv = lax.all_to_all(
        jnp.concatenate(
            [keys.reshape(devices, heads_kv, DH), values.reshape(devices, heads_kv, DH)], axis=1
        ),
        "seq",
        split_axis=0,
        concat_axis=0,
        tiled=True,
    )
    q_heads = arrived_q.transpose(1, 0, 2)
    own_q0 = arrived_q[0].reshape(-1, 2 * width_k)
    kv = jnp.concatenate([arrived_kv.reshape(row_count, 2 * width_k), own_q0], axis=0)
    owner_doc, first_block = block_docs(lengths, devices)
    my_doc = owner_doc[myself]
    reach = MAXB - 1
    pieces = [kv]
    flags = [jnp.ones((), jnp.int32)]
    firsts = [own_q0]
    right = kv
    left = kv
    for hop in range(1, reach + 1):
        right = shifted(right, "seq", 1)
        left = shifted(left, "seq", -1)
        firsts.append(right[row_count:])
        for piece, source in ((right, myself - hop), (left, myself + hop)):
            inside = (source >= 0) & (source < devices)
            clipped = jnp.clip(source, 0, devices - 1)
            pieces.append(piece)
            flags.append((inside & (owner_doc[clipped] == my_doc)).astype(jnp.int32))
    distance = jnp.clip(myself - first_block[myself], 0, reach)
    start_q0 = lax.dynamic_index_in_dim(jnp.stack(firsts), distance, 0, False)
    q0t = start_q0.reshape(heads_kv, group, DH).transpose(0, 2, 1)
    q0t = jnp.pad(q0t, ((0, 0), (0, 0), (0, DH - group)))
    attended, start_out = attend(jnp.stack(flags), q_heads, q0t, pieces)
    start_row = start_out[:, :, :group].transpose(0, 2, 1).reshape(1, width_q).astype(jnp.bfloat16)
    doc_logits = jnp.dot(start_row, class_weight, preferred_element_type=jnp.float32)
    return (attended, doc_logits)


def solution(mesh):
    return jax.shard_map(
        shards,
        mesh=mesh,
        in_specs=(P("seq", None), P("seq", None), P("seq", None), P(), P()),
        out_specs=(P("seq", None), P("seq", None)),
        check_vma=False,
    )
```

time: 262 us -> 241 us (0.920)
  the two profiles are of different devices: /device:TPU:51 before, /device:TPU:119 now
where the time goes in v3:
time: 241 us
  starting transfers between devices  92.6 us (38%)
  waiting for transfers between devices  60.8 us (25%)
  Pallas kernels  49.2 us (20%)
  between operations  18.5 us (8%)
  local copies, waits for them, and re-layouts  17.8 us (7%)
    ppermute x14, starting transfers between devices, shifted(): return lax.ppermute(block, axis, route)  72.1 us
    pallas_call x1, Pallas kernels, attend(): pl.pallas_call(attention_kernel, out_shape=(jax.ShapeDtypeStruct((rows, h...  49.2 us
    ppermute x14, waiting for transfers between devices, shifted(): return lax.ppermute(block, axis, route)  35.4 us
    all_to_all x1, waiting for transfers between devices, shards(): lax.all_to_all(queries.reshape(devices, heads, DH), 'seq', split_axis=0,...  23.6 us
    all_to_all x1, starting transfers between devices, shards(): lax.all_to_all(queries.reshape(devices, heads, DH), 'seq', split_axis=0,...  10.5 us
    all_to_all x1, starting transfers between devices, shards(): lax.all_to_all(jnp.concatenate([keys.reshape(devices, heads_kv, DH), valu...  10 us
    unnamed x35, local copies, waits for them, and re-layouts  8.57 us
  transfers between devices with their start and end apart: 16, of which 12 were waited for; matrix products, arithmetic and copies ran while one was open for 6% of the time, Pallas kernels for 0%

profile of v3, /device:TPU:119, one launch (start us, length us, event | category | flops | bytes accessed | tf_op | source)
XLA Modules:
  0.0 241.4 jit_solution(16786875612607474755)
XLA Ops:
  3.6 10.0 %all-to-all-start.1 = ((bf16[128,16,128]{2,1,0:T(8,128)(2,1)}), bf16[128,16,128]{2,1,0:T(8,128)(2,1)S(1)}, u32[]{:S(2)}, u32[]{:S(2)}) async-start(bf16[128,16,128]{2,1,0:T(8,128)(2,1)} %pad_maximum_fusion), calls=%async_computation.1 | async-start | bytes 1048576 | tf_op jit(solution)/shard_map/all_to_all | solution.py:140
  13.6 3.2 %copy.20 = bf16[128,8192]{0,1:T(8,128)(2,1)S(1)} copy(bf16[128,8192]{1,0:T(8,128)(2,1)} %param.5) | data formatting | bytes 4194304 | tf_op args[0]
  16.8 2.8 %copy.21 = bf16[128,64,128]{2,1,0:T(8,128)(2,1)} copy(bf16[128,64,128]{0,2,1:T(8,128)(2,1)S(1)} %bitcast.76) | data formatting | bytes 4194304 | tf_op jit(solution)/shard_map/reshape | solution.py:138
  21.4 10.5 %all-to-all-start = ((bf16[128,64,128]{2,1,0:T(8,128)(2,1)}), bf16[128,64,128]{2,1,0:T(8,128)(2,1)S(1)}, u32[]{:S(2)}, u32[]{:S(2)}) async-start(bf16[128,64,128]{2,1,0:T(8,128)(2,1)} %copy.21), calls=%async_computation | async-start | bytes 4194304 | tf_op jit(solution)/shard_map/all_to_all | solution.py:137
  32.1 23.6 %all-to-all-done = bf16[128,64,128]{2,1,0:T(8,128)(2,1)S(1)} async-done(((bf16[128,64,128]{2,1,0:T(8,128)(2,1)}), bf16[128,64,128]{2,1,0:T(8,128)(2,1)S(1)}, u32[]{:S(2)}, u32[]{:S(2)}) %all-to-all-start) | async-done | bytes 2097184 | tf_op jit(solution)/shard_map/all_to_all | solution.py:137
  55.7 7.8 %collective-permute-start = (bf16[132,2048]{1,0:T(8,128)(2,1)S(1)}, bf16[132,2048]{1,0:T(8,128)(2,1)S(1)}, u32[]{:S(2)}, u32[]{:S(2)}) collective-permute-start(bf16[132,2048]{1,0:T(8,128)(2,1)S(1)} %constant_dynamic-update-slice_fusion.refs_0_), channel_id=1, source_target_pairs={{0,1},{1,2},{2,3},{3,4},{4,5},{5,6},{6,7},{7,8},{8,9},{9,10},{10,1... | collective-permute-start | bytes 1622024 | tf_op jit(solution)/shard_map/ppermute | solution.py:19
  63.6 1.9 collective-permute-start.7
  65.5 4.5 %collective-permute-done.refs_1_ = bf16[132,2048]{1,0:T(8,128)(2,1)S(1)} collective-permute-done((bf16[132,2048]{1,0:T(8,128)(2,1)S(1)}, bf16[132,2048]{1,0:T(8,128)(2,1)S(1)}, u32[]{:S(2)}, u32[]{:S(2)}) %collective-permute-start) | collective-permute-done | bytes 540704 | tf_op jit(solution)/shard_map/ppermute | solution.py:19
  70.0 8.6 %collective-permute-start.1 = (bf16[132,2048]{1,0:T(8,128)(2,1)S(1)}, bf16[132,2048]{1,0:T(8,128)(2,1)S(1)}, u32[]{:S(2)}, u32[]{:S(2)}) collective-permute-start(bf16[132,2048]{1,0:T(8,128)(2,1)S(1)} %collective-permute-done.refs_1_), channel_id=1, source_target_pairs={{0,1},{1,2},{2,3},{3,4},{4,5},{5,6},{6,7},{7,8},{8,9},{9,10},{10,1... | collective-permute-start | bytes 1622024 | tf_op jit(solution)/shard_map/ppermute | solution.py:19
  78.6 1.9 collective-permute-start.8
  80.6 4.5 %collective-permute-done.1.refs_3_ = bf16[132,2048]{1,0:T(8,128)(2,1)S(1)} collective-permute-done((bf16[132,2048]{1,0:T(8,128)(2,1)S(1)}, bf16[132,2048]{1,0:T(8,128)(2,1)S(1)}, u32[]{:S(2)}, u32[]{:S(2)}) %collective-permute-start.1) | collective-permute-done | bytes 540704 | tf_op jit(solution)/shard_map/ppermute | solution.py:19
  85.9 8.6 %collective-permute-start.2 = (bf16[132,2048]{1,0:T(8,128)(2,1)S(1)}, bf16[132,2048]{1,0:T(8,128)(2,1)}, u32[]{:S(2)}, u32[]{:S(2)}) collective-permute-start(bf16[132,2048]{1,0:T(8,128)(2,1)S(1)} %collective-permute-done.1.refs_3_), channel_id=1, source_target_pairs={{0,1},{1,2},{2,3},{3,4},{4,5},{5,6},{6,7},{7,8},{8,9},{9,10},{10,1... | collective-permute-start | bytes 1622024 | tf_op jit(solution)/shard_map/ppermute | solution.py:19
  94.5 1.9 collective-permute-start.9
  96.4 4.5 %collective-permute-done.2.refs_5_ = bf16[132,2048]{1,0:T(8,128)(2,1)} collective-permute-done((bf16[132,2048]{1,0:T(8,128)(2,1)S(1)}, bf16[132,2048]{1,0:T(8,128)(2,1)}, u32[]{:S(2)}, u32[]{:S(2)}) %collective-permute-start.2) | collective-permute-done | bytes 540704 | tf_op jit(solution)/shard_map/ppermute | solution.py:19
  100.9 8.7 %collective-permute-start.3 = (bf16[132,2048]{1,0:T(8,128)(2,1)}, bf16[132,2048]{1,0:T(8,128)(2,1)}, u32[]{:S(2)}, u32[]{:S(2)}) collective-permute-start(bf16[132,2048]{1,0:T(8,128)(2,1)} %collective-permute-done.2.refs_5_), channel_id=1, source_target_pairs={{0,1},{1,2},{2,3},{3,4},{4,5},{5,6},{6,7},{7,8},{8,9},{9,10},{10,1... | collective-permute-start | bytes 1622024 | tf_op jit(solution)/shard_map/ppermute | solution.py:19
  131.6 2.7 %copy.30 = bf16[128,64,128]{2,0,1:T(8,128)(2,1)} copy(bf16[128,64,128]{2,1,0:T(8,128)(2,1)S(1)} %all-to-all-done) | data formatting | bytes 4194304 | tf_op jit(solution)/shard_map/all_to_all | solution.py:137
  134.3 7.8 %collective-permute-start.4 = (bf16[132,2048]{1,0:T(8,128)(2,1)}, bf16[132,2048]{1,0:T(8,128)(2,1)S(1)}, u32[]{:S(2)}, u32[]{:S(2)}) collective-permute-start(bf16[132,2048]{1,0:T(8,128)(2,1)} %collective-permute-done.3.refs_7_), channel_id=1, source_target_pairs={{0,1},{1,2},{2,3},{3,4},{4,5},{5,6},{6,7},{7,8},{8,9},{9,10},{10,1... | collective-permute-start | bytes 1622024 | tf_op jit(solution)/shard_map/ppermute | solution.py:19
  142.2 2.8 %collective-permute-done.10.refs_8_ = bf16[132,2048]{1,0:T(8,128)(2,1)S(1)} collective-permute-done((bf16[132,2048]{1,0:T(8,128)(2,1)}, bf16[132,2048]{1,0:T(8,128)(2,1)S(1)}, u32[]{:S(2)}, u32[]{:S(2)}) %collective-permute-start.10) | collective-permute-done | bytes 540704 | tf_op jit(solution)/shard_map/ppermute | solution.py:19
  149.0 8.5 %collective-permute-start.5 = (bf16[132,2048]{1,0:T(8,128)(2,1)S(1)}, bf16[132,2048]{1,0:T(8,128)(2,1)S(1)}, u32[]{:S(2)}, u32[]{:S(2)}) collective-permute-start(bf16[132,2048]{1,0:T(8,128)(2,1)S(1)} %collective-permute-done.4.refs_9_), channel_id=1, source_target_pairs={{0,1},{1,2},{2,3},{3,4},{4,5},{5,6},{6,7},{7,8},{8,9},{9,10},{10,1... | collective-permute-start | bytes 1622024 | tf_op jit(solution)/shard_map/ppermute | solution.py:19
  163.9 8.6 %collective-permute-start.6 = (bf16[132,2048]{1,0:T(8,128)(2,1)S(1)}, bf16[132,2048]{1,0:T(8,128)(2,1)S(1)}, u32[]{:S(2)}, u32[]{:S(2)}) collective-permute-start(bf16[132,2048]{1,0:T(8,128)(2,1)S(1)} %collective-permute-done.5.refs_11_), channel_id=1, source_target_pairs={{0,1},{1,2},{2,3},{3,4},{4,5},{5,6},{6,7},{7,8},{8,9},{9,10},{10,1... | collective-permute-start | bytes 1622024 | tf_op jit(solution)/shard_map/ppermute | solution.py:19
  172.5 2.5 %collective-permute-done.12.refs_12_ = bf16[132,2048]{1,0:T(8,128)(2,1)S(1)} collective-permute-done((bf16[132,2048]{1,0:T(8,128)(2,1)S(1)}, bf16[132,2048]{1,0:T(8,128)(2,1)S(1)}, u32[]{:S(2)}, u32[]{:S(2)}) %collective-permute-start.12) | collective-permute-done | bytes 540704 | tf_op jit(solution)/shard_map/ppermute | solution.py:19
  177.0 1.9 collective-permute-done.6.refs_13_
  180.0 10.3 %collective-permute-done.13.refs_14_ = bf16[132,2048]{1,0:T(8,128)(2,1)} collective-permute-done((bf16[132,2048]{1,0:T(8,128)(2,1)S(1)}, bf16[132,2048]{1,0:T(8,128)(2,1)}, u32[]{:S(2)}, u32[]{:S(2)}) %collective-permute-start.13) | collective-permute-done | bytes 540704 | tf_op jit(solution)/shard_map/ppermute | solution.py:19
  190.3 49.2 %shard_map.68 = (bf16[128,8192]{1,0:T(8,128)(2,1)}, f32[8,128,128]{2,1,0:T(8,128)}) custom-call(s32[15]{0:T(128)} %stack.100.flags_ref, bf16[64,128,128]{2,1,0:T(8,128)(2,1)} %bitcast.77, bf16[8,128,128]{2,1,0:T(8,128)(2,1)} %pad.4.q0t_ref, bf16[132,2048]{1,0:T(8,128)(2,1)} %copy-done.1, bf16[132,2048]{1,0:T(8,128)(2,1)} %copy-done.2, ...), custom_call_target="tpu_custom_call" | custom-call | tf_op jit(solution)/shard_map/pallas_call | solution.py:106
  (70 shorter events, 25.4 us)
Async XLA Ops:
  0.6 240.1 %copy-start = (bf16[8192,16]{0,1:T(8,128)(2,1)S(1)}, bf16[8192,16]{0,1:T(8,128)(2,1)}, u32[]{:S(2)}) copy-start(bf16[8192,16]{0,1:T(8,128)(2,1)} %param.9) | copy-start | bytes 786436
  3.6 17.8 %all-to-all-start.1 = ((bf16[128,16,128]{2,1,0:T(8,128)(2,1)}), bf16[128,16,128]{2,1,0:T(8,128)(2,1)S(1)}, u32[]{:S(2)}, u32[]{:S(2)}) async-start(bf16[128,16,128]{2,1,0:T(8,128)(2,1)} %pad_maximum_fusion), calls=%async_computation.1 | async-start | bytes 1048576 | tf_op jit(solution)/shard_map/all_to_all | solution.py:140
  19.6 90.1 %copy-start.11 = (s32[32]{0:T(128)S(1)}, s32[32]{0:T(128)}, u32[]{:S(2)}) copy-start(s32[32]{0:T(128)} %param.8) | copy-start | bytes 388
  21.4 34.3 %all-to-all-start = ((bf16[128,64,128]{2,1,0:T(8,128)(2,1)}), bf16[128,64,128]{2,1,0:T(8,128)(2,1)S(1)}, u32[]{:S(2)}, u32[]{:S(2)}) async-start(bf16[128,64,128]{2,1,0:T(8,128)(2,1)} %copy.21), calls=%async_computation | async-start | bytes 4194304 | tf_op jit(solution)/shard_map/all_to_all | solution.py:137
  55.7 78.6 %copy-start.1 = (bf16[132,2048]{1,0:T(8,128)(2,1)}, bf16[132,2048]{1,0:T(8,128)(2,1)S(1)}, u32[]{:S(2)}) copy-start(bf16[132,2048]{1,0:T(8,128)(2,1)S(1)} %constant_dynamic-update-slice_fusion.refs_0_) | copy-start | bytes 1622020
  55.7 14.3 %collective-permute-start = (bf16[132,2048]{1,0:T(8,128)(2,1)S(1)}, bf16[132,2048]{1,0:T(8,128)(2,1)S(1)}, u32[]{:S(2)}, u32[]{:S(2)}) collective-permute-start(bf16[132,2048]{1,0:T(8,128)(2,1)S(1)} %constant_dynamic-update-slice_fusion.refs_0_), channel_id=1, source_target_pairs={{0,1},{1,2},{2,3},{3,4},{4,5},{5,6},{6,7},{7,8},{8,9},{9,10},{10,1... | collective-permute-start | bytes 1622024 | tf_op jit(solution)/shard_map/ppermute | solution.py:19
  63.6 15.1 %collective-permute-start.7 = (bf16[132,2048]{1,0:T(8,128)(2,1)S(1)}, bf16[132,2048]{1,0:T(8,128)(2,1)S(1)}, u32[]{:S(2)}, u32[]{:S(2)}) collective-permute-start(bf16[132,2048]{1,0:T(8,128)(2,1)S(1)} %constant_dynamic-update-slice_fusion.refs_0_), channel_id=1, source_target_pairs={{1,0},{2,1},{3,2},{4,3},{5,4},{6,5},{7,6},{8,7},{9,8},{10,9},{11,1... | collective-permute-start | bytes 1622024 | tf_op jit(solution)/shard_map/ppermute | solution.py:19
  70.0 72.2 %copy-start.2 = (bf16[132,2048]{1,0:T(8,128)(2,1)}, bf16[132,2048]{1,0:T(8,128)(2,1)S(1)}, u32[]{:S(2)}) copy-start(bf16[132,2048]{1,0:T(8,128)(2,1)S(1)} %collective-permute-done.refs_1_) | copy-start | bytes 1622020
  70.0 15.1 %collective-permute-start.1 = (bf16[132,2048]{1,0:T(8,128)(2,1)S(1)}, bf16[132,2048]{1,0:T(8,128)(2,1)S(1)}, u32[]{:S(2)}, u32[]{:S(2)}) collective-permute-start(bf16[132,2048]{1,0:T(8,128)(2,1)S(1)} %collective-permute-done.refs_1_), channel_id=1, source_target_pairs={{0,1},{1,2},{2,3},{3,4},{4,5},{5,6},{6,7},{7,8},{8,9},{9,10},{10,1... | collective-permute-start | bytes 1622024 | tf_op jit(solution)/shard_map/ppermute | solution.py:19
  78.6 15.8 %collective-permute-start.8 = (bf16[132,2048]{1,0:T(8,128)(2,1)S(1)}, bf16[132,2048]{1,0:T(8,128)(2,1)}, u32[]{:S(2)}, u32[]{:S(2)}) collective-permute-start(bf16[132,2048]{1,0:T(8,128)(2,1)S(1)} %collective-permute-done.7.refs_2_), channel_id=1, source_target_pairs={{1,0},{2,1},{3,2},{4,3},{5,4},{6,5},{7,6},{8,7},{9,8},{10,9},{11,1... | collective-permute-start | bytes 1622024 | tf_op jit(solution)/shard_map/ppermute | solution.py:19
  85.9 15.1 %collective-permute-start.2 = (bf16[132,2048]{1,0:T(8,128)(2,1)S(1)}, bf16[132,2048]{1,0:T(8,128)(2,1)}, u32[]{:S(2)}, u32[]{:S(2)}) collective-permute-start(bf16[132,2048]{1,0:T(8,128)(2,1)S(1)} %collective-permute-done.1.refs_3_), channel_id=1, source_target_pairs={{0,1},{1,2},{2,3},{3,4},{4,5},{5,6},{6,7},{7,8},{8,9},{9,10},{10,1... | collective-permute-start | bytes 1622024 | tf_op jit(solution)/shard_map/ppermute | solution.py:19
  94.5 35.2 %collective-permute-start.9 = (bf16[132,2048]{1,0:T(8,128)(2,1)}, bf16[132,2048]{1,0:T(8,128)(2,1)}, u32[]{:S(2)}, u32[]{:S(2)}) collective-permute-start(bf16[132,2048]{1,0:T(8,128)(2,1)} %collective-permute-done.8.refs_4_), channel_id=1, source_target_pairs={{1,0},{2,1},{3,2},{4,3},{5,4},{6,5},{7,6},{8,7},{9,8},{10,9},{11,1... | collective-permute-start | bytes 1622024 | tf_op jit(solution)/shard_map/ppermute | solution.py:19
  100.9 33.4 %collective-permute-start.3 = (bf16[132,2048]{1,0:T(8,128)(2,1)}, bf16[132,2048]{1,0:T(8,128)(2,1)}, u32[]{:S(2)}, u32[]{:S(2)}) collective-permute-start(bf16[132,2048]{1,0:T(8,128)(2,1)} %collective-permute-done.2.refs_5_), channel_id=1, source_target_pairs={{0,1},{1,2},{2,3},{3,4},{4,5},{5,6},{6,7},{7,8},{8,9},{9,10},{10,1... | collective-permute-start | bytes 1622024 | tf_op jit(solution)/shard_map/ppermute | solution.py:19
  129.7 15.3 %collective-permute-start.10 = (bf16[132,2048]{1,0:T(8,128)(2,1)}, bf16[132,2048]{1,0:T(8,128)(2,1)S(1)}, u32[]{:S(2)}, u32[]{:S(2)}) collective-permute-start(bf16[132,2048]{1,0:T(8,128)(2,1)} %collective-permute-done.9.refs_6_), channel_id=1, source_target_pairs={{1,0},{2,1},{3,2},{4,3},{5,4},{6,5},{7,6},{8,7},{9,8},{10,9},{11,1... | collective-permute-start | bytes 1622024 | tf_op jit(solution)/shard_map/ppermute | solution.py:19
  134.3 14.6 %collective-permute-start.4 = (bf16[132,2048]{1,0:T(8,128)(2,1)}, bf16[132,2048]{1,0:T(8,128)(2,1)S(1)}, u32[]{:S(2)}, u32[]{:S(2)}) collective-permute-start(bf16[132,2048]{1,0:T(8,128)(2,1)} %collective-permute-done.3.refs_7_), channel_id=1, source_target_pairs={{0,1},{1,2},{2,3},{3,4},{4,5},{5,6},{6,7},{7,8},{8,9},{9,10},{10,1... | collective-permute-start | bytes 1622024 | tf_op jit(solution)/shard_map/ppermute | solution.py:19
  145.0 34.0 %copy-start.8 = (bf16[132,2048]{1,0:T(8,128)(2,1)}, bf16[132,2048]{1,0:T(8,128)(2,1)S(1)}, u32[]{:S(2)}) copy-start(bf16[132,2048]{1,0:T(8,128)(2,1)S(1)} %collective-permute-done.10.refs_8_) | copy-start | bytes 1622020
  145.0 15.1 %collective-permute-start.11 = (bf16[132,2048]{1,0:T(8,128)(2,1)S(1)}, bf16[132,2048]{1,0:T(8,128)(2,1)S(1)}, u32[]{:S(2)}, u32[]{:S(2)}) collective-permute-start(bf16[132,2048]{1,0:T(8,128)(2,1)S(1)} %collective-permute-done.10.refs_8_), channel_id=1, source_target_pairs={{1,0},{2,1},{3,2},{4,3},{5,4},{6,5},{7,6},{8,7},{9,8},{10,9},{11,1... | collective-permute-start | bytes 1622024 | tf_op jit(solution)/shard_map/ppermute | solution.py:19
  149.0 41.3 %copy-start.4 = (bf16[132,2048]{1,0:T(8,128)(2,1)}, bf16[132,2048]{1,0:T(8,128)(2,1)S(1)}, u32[]{:S(2)}) copy-start(bf16[132,2048]{1,0:T(8,128)(2,1)S(1)} %collective-permute-done.4.refs_9_) | copy-start | bytes 1622020
  149.0 15.0 %collective-permute-start.5 = (bf16[132,2048]{1,0:T(8,128)(2,1)S(1)}, bf16[132,2048]{1,0:T(8,128)(2,1)S(1)}, u32[]{:S(2)}, u32[]{:S(2)}) collective-permute-start(bf16[132,2048]{1,0:T(8,128)(2,1)S(1)} %collective-permute-done.4.refs_9_), channel_id=1, source_target_pairs={{0,1},{1,2},{2,3},{3,4},{4,5},{5,6},{6,7},{7,8},{8,9},{9,10},{10,1... | collective-permute-start | bytes 1622024 | tf_op jit(solution)/shard_map/ppermute | solution.py:19
  160.0 30.2 %copy-start.9 = (bf16[132,2048]{1,0:T(8,128)(2,1)}, bf16[132,2048]{1,0:T(8,128)(2,1)S(1)}, u32[]{:S(2)}) copy-start(bf16[132,2048]{1,0:T(8,128)(2,1)S(1)} %collective-permute-done.11.refs_10_) | copy-start | bytes 1622020
  160.0 15.1 %collective-permute-start.12 = (bf16[132,2048]{1,0:T(8,128)(2,1)S(1)}, bf16[132,2048]{1,0:T(8,128)(2,1)S(1)}, u32[]{:S(2)}, u32[]{:S(2)}) collective-permute-start(bf16[132,2048]{1,0:T(8,128)(2,1)S(1)} %collective-permute-done.11.refs_10_), channel_id=1, source_target_pairs={{1,0},{2,1},{3,2},{4,3},{5,4},{6,5},{7,6},{8,7},{9,8},{10,9},{11,1... | collective-permute-start | bytes 1622024 | tf_op jit(solution)/shard_map/ppermute | solution.py:19
  163.9 26.4 %copy-start.5 = (bf16[132,2048]{1,0:T(8,128)(2,1)}, bf16[132,2048]{1,0:T(8,128)(2,1)S(1)}, u32[]{:S(2)}) copy-start(bf16[132,2048]{1,0:T(8,128)(2,1)S(1)} %collective-permute-done.5.refs_11_) | copy-start | bytes 1622020
  163.9 15.1 %collective-permute-start.6 = (bf16[132,2048]{1,0:T(8,128)(2,1)S(1)}, bf16[132,2048]{1,0:T(8,128)(2,1)S(1)}, u32[]{:S(2)}, u32[]{:S(2)}) collective-permute-start(bf16[132,2048]{1,0:T(8,128)(2,1)S(1)} %collective-permute-done.5.refs_11_), channel_id=1, source_target_pairs={{0,1},{1,2},{2,3},{3,4},{4,5},{5,6},{6,7},{7,8},{8,9},{9,10},{10,1... | collective-permute-start | bytes 1622024 | tf_op jit(solution)/shard_map/ppermute | solution.py:19
  175.1 15.2 %collective-permute-start.13 = (bf16[132,2048]{1,0:T(8,128)(2,1)S(1)}, bf16[132,2048]{1,0:T(8,128)(2,1)}, u32[]{:S(2)}, u32[]{:S(2)}) collective-permute-start(bf16[132,2048]{1,0:T(8,128)(2,1)S(1)} %collective-permute-done.12.refs_12_), channel_id=1, source_target_pairs={{1,0},{2,1},{3,2},{4,3},{5,4},{6,5},{7,6},{8,7},{9,8},{10,9},{11,1... | collective-permute-start | bytes 1622024 | tf_op jit(solution)/shard_map/ppermute | solution.py:19
  (4 other events, 49.6 us)
